TPU v7x, 1024 devices: a whole 8x8x8 slice. The times are simulated.
1024 devices in a mesh: expert: 8 (over x), dp: 128 (over y, z, core).
Axes of the slice: x: 8, y: 8, z: 8, core: 2. Of those that a mesh axis runs over, the one named last changes fastest.
Arguments:
- hidden: bfloat16 [131072, 768], P(('expert', 'dp')), may hold values from -24 to 24
- cotangent: bfloat16 [131072, 1024], P(('expert', 'dp')), may hold values from -6 to 6
- expert_ids: int32 [131072, 1], P(('expert', 'dp')), may hold values from 0 to 7; in each aligned block of 128 rows (0 to 127, 128 to 255, ...) at most 32 rows name the same one
- counts: int32 [8, 128], P('expert', 'dp'), may hold values from 64 to 128, as said below
- down_weight: bfloat16 [8, 768, 1024], P('expert', 'dp'), may hold values from -0.21875 to 0.21875
Outputs:
- output: bfloat16 [131072, 1024], P(('expert', 'dp'))
- hidden_grad: bfloat16 [131072, 768], P(('expert', 'dp'))
- weight_grad: float32 [8, 768, 1024], P('expert', 'dp')
Inputs may be any that keep to these rules, and one draw needn't show every extreme that they name: `expert_ids`: in the rows of one device no expert is named more than 32 times, and some device names some expert exactly 32 times. `counts`: some device is full in every draw.
All inputs are finite; a program needn't handle non-finite values.
Results may differ from a plain program's by a relative error of at most 0.001.
Values may be sent and summed in bfloat16 or wider, within the bound.
No kernel may reach another device: no remote copies, remote signals or barrier semaphores. Data moves between devices by JAX's collectives and lax.ppermute only.
A program may use at most 32 MiB of HBM per device.

v0:
```python
import jax
import jax.numpy as jnp
from jax import lax
from jax.sharding import PartitionSpec as P

CAP = 32


def on_device(hidden, cotangent, expert_ids, counts, down_weight):
    tok_rows = hidden.shape[0]
    groups = lax.axis_size("expert")
    width = groups * CAP
    ids = expert_ids[:, 0]
    live = jnp.arange(tok_rows, dtype=jnp.int32) < counts[0, 0]
    member = (ids[:, None] == jnp.arange(groups, dtype=jnp.int32)[None, :]).astype(jnp.int32)
    rank = jnp.sum((jnp.cumsum(member, 0) - 1) * member, 1)
    target = ids * CAP + rank
    placing = jnp.logical_and(
        target[None, :] == jnp.arange(width, dtype=jnp.int32)[:, None], live[None, :]
    ).astype(jnp.bfloat16)
    h_send = (
        jnp.dot(placing, hidden, preferred_element_type=jnp.float32)
        .astype(jnp.bfloat16)
        .reshape(groups, CAP, -1)
    )
    g_send = (
        jnp.dot(placing, cotangent, preferred_element_type=jnp.float32)
        .astype(jnp.bfloat16)
        .reshape(groups, CAP, -1)
    )
    weight = lax.all_gather(down_weight, "dp", axis=1, tiled=True)[0]
    h_recv = lax.all_to_all(h_send, "expert", split_axis=0, concat_axis=0, tiled=True)
    rows = h_recv.reshape(width, -1)
    y_back = lax.all_to_all(
        jnp.dot(rows, weight, preferred_element_type=jnp.float32)
        .astype(jnp.bfloat16)
        .reshape(groups, CAP, -1),
        "expert",
        split_axis=0,
        concat_axis=0,
        tiled=True,
    )
    g_recv = lax.all_to_all(g_send, "expert", split_axis=0, concat_axis=0, tiled=True)
    rows = g_recv.reshape(width, -1)
    result = lax.dot_general(
        rows, weight, (((1,), (1,)), ((), ())), preferred_element_type=jnp.float32
    )
    dh_back = lax.all_to_all(
        result.astype(jnp.bfloat16).reshape(groups, CAP, -1),
        "expert",
        split_axis=0,
        concat_axis=0,
        tiled=True,
    )
    output = lax.dot_general(
        placing,
        y_back.reshape(width, -1),
        (((0,), (0,)), ((), ())),
        preferred_element_type=jnp.float32,
    ).astype(jnp.bfloat16)
    hidden_grad = lax.dot_general(
        placing,
        dh_back.reshape(width, -1),
        (((0,), (0,)), ((), ())),
        preferred_element_type=jnp.float32,
    ).astype(jnp.bfloat16)
    h_rows = h_recv.reshape(width, -1)
    g_rows = g_recv.reshape(width, -1)
    partial_grad = lax.dot_general(
        h_rows, g_rows, (((0,), (0,)), ((), ())), preferred_element_type=jnp.float32
    )
    summed = lax.psum_scatter(partial_grad, "dp", scatter_dimension=1, tiled=True)
    shard_rows = lax.all_to_all(summed, "dp", split_axis=0, concat_axis=1, tiled=True)
    return (output, hidden_grad, shard_rows[None])


def solution(mesh):
    placed = (
        P(("expert", "dp"), None),
        P(("expert", "dp"), None),
        P(("expert", "dp"), None),
        P("expert", "dp"),
        P("expert", "dp", None),
    )
    return jax.shard_map(
        on_device,
        mesh=mesh,
        in_specs=placed,
        out_specs=(P(("expert", "dp"), None), P(("expert", "dp"), None), P("expert", "dp", None)),
        check_vma=False,
    )
```

profile of v0, /device:TPU:1, one launch (start us, length us, event | category | flops | bytes accessed | tf_op | source)
XLA Modules:
  0.0 368.4 jit_solution(3821515155322124962)
XLA Ops:
  7.2 0.0 copy-start
  7.2 0.0 all-gather.2.cloned.1.call-start
  7.2 1.4 copy.15
  8.6 0.0 all-gather.2.cloned.1.call-update
  9.3 0.7 fusion.21
  10.0 0.2 reduce_window_sum.11
  10.2 0.8 select_reduce_fusion
  11.0 0.7 multiply_add_fusion
  11.7 1.9 convolution_convert_fusion.1
  13.6 7.3 %all-to-all-start = ((bf16[8,32,768]{2,1,0:T(8,128)(2,1)}), bf16[8,32,768]{2,1,0:T(8,128)(2,1)S(1)}, u32[]{:S(2)}, u32[]{:S(2)}) async-start(bf16[8,32,768]{2,1,0:T(8,128)(2,1)} %bitcast.2), calls=%async_computation | async-start | bytes 786432 | tf_op jit(solution)/shard_map/all_to_all | solution.py:32
  20.9 0.0 reduce-scatter.2.cloned.1.call-start
  21.0 0.0 copy-done
  21.0 0.3 convolution_convert_fusion
  21.3 10.4 %all-to-all-done = bf16[8,32,768]{2,1,0:T(8,128)(2,1)S(1)} async-done(((bf16[8,32,768]{2,1,0:T(8,128)(2,1)}), bf16[8,32,768]{2,1,0:T(8,128)(2,1)S(1)}, u32[]{:S(2)}, u32[]{:S(2)}) %all-to-all-start) | async-done | bytes 393248 | tf_op jit(solution)/shard_map/all_to_all | solution.py:32
  31.7 16.3 %all_to_all.36 = bf16[8,32,1024]{2,1,0:T(8,128)(2,1)S(1)} all-to-all(bf16[8,32,1024]{2,1,0:T(8,128)(2,1)S(1)} %bitcast.38), channel_id=1, replica_groups=mesh['expert'=8,'dp'=128] {'expert'}, dimensions={0} | all-to-all | bytes 1048576 | tf_op jit(solution)/shard_map/all_to_all | solution.py:43
  48.0 2.3 convolution_bitcast_fusion
  50.3 0.0 reduce-scatter.2.cloned.1.call-update
  50.3 66.5 %all-gather.2.cloned.1.call-done = bf16[1,768,1024]{2,0,1:T(2,128)(2,1)} async-done(((bf16[1,6,1024]{2,0,1:T(2,128)(2,1)}), bf16[1,768,1024]{2,0,1:T(2,128)(2,1)}) %all-gather.2.cloned.1.call-update) | async-done | bytes 1572880 | tf_op jit(solution)/shard_map/all_gather | solution.py:31
  116.7 3.4 fusion.7
  120.1 6.4 %all-to-all-start.3 = ((bf16[8,32,768]{2,1,0:T(8,128)(2,1)}), bf16[8,32,768]{2,1,0:T(8,128)(2,1)S(1)}, u32[]{:S(2)}, u32[]{:S(2)}) async-start(bf16[8,32,768]{2,1,0:T(8,128)(2,1)} %bitcast.8), calls=%async_computation.3 | async-start | bytes 786432 | tf_op jit(solution)/shard_map/all_to_all | solution.py:48
  126.5 3.4 fusion.4
  129.9 11.8 %all-to-all-done.3 = bf16[8,32,768]{2,1,0:T(8,128)(2,1)S(1)} async-done(((bf16[8,32,768]{2,1,0:T(8,128)(2,1)}), bf16[8,32,768]{2,1,0:T(8,128)(2,1)S(1)}, u32[]{:S(2)}, u32[]{:S(2)}) %all-to-all-start.3) | async-done | bytes 393248 | tf_op jit(solution)/shard_map/all_to_all | solution.py:48
  141.7 3.5 all-to-all-start.1
  145.2 0.9 convolution_convert_fusion.3
  146.1 178.5 %reduce-scatter.2.cloned.1.call-done = f32[768,8]{0,1:T(8,128)} async-done(((f32[768,1024]{0,1:T(8,128)}), f32[768,8]{0,1:T(8,128)}) %reduce-scatter.2.cloned.1.call-update) | async-done | bytes 24592 | tf_op jit(solution)/shard_map/reduce_scatter | solution.py:72
  324.6 1.2 all_to_all.28
  325.8 1.1 copy.16
  326.9 0.0 all-to-all-done.1
  326.9 14.3 %all-to-all-start.4 = ((f32[128,6,8]{1,2,0:T(8,128)}), f32[128,6,8]{1,2,0:T(8,128)S(1)}, u32[]{:S(2)}, u32[]{:S(2)}) async-start(f32[128,6,8]{1,2,0:T(8,128)} %copy.16), calls=%async_computation.5 | async-start | bytes 1048576 | tf_op jit(solution)/shard_map/all_to_all | solution.py:73
  341.3 1.0 convolution_convert_fusion.2
  342.2 18.5 %all-to-all-done.4 = f32[128,6,8]{1,2,0:T(8,128)S(1)} async-done(((f32[128,6,8]{1,2,0:T(8,128)}), f32[128,6,8]{1,2,0:T(8,128)S(1)}, u32[]{:S(2)}, u32[]{:S(2)}) %all-to-all-start.4) | async-done | bytes 24608 | tf_op jit(solution)/shard_map/all_to_all | solution.py:73
  360.7 0.8 copy.18
  (1 shorter events, 0.0 us)
Async XLA Ops:
  7.2 13.8 %copy-start = (bf16[128,1024]{1,0:T(8,128)(2,1)S(1)}, bf16[128,1024]{1,0:T(8,128)(2,1)}, u32[]{:S(2)}) copy-start(bf16[128,1024]{1,0:T(8,128)(2,1)} %param.6) | copy-start | bytes 786436
  7.2 109.6 %all-gather.2.cloned.1.call-start = ((), (), s32[]{:S(2)}) async-start(), calls=%async_computation.6 | async-start | bytes 3170304 | tf_op jit(solution)/shard_map/all_gather | solution.py:31
  13.6 18.0 %all-to-all-start = ((bf16[8,32,768]{2,1,0:T(8,128)(2,1)}), bf16[8,32,768]{2,1,0:T(8,128)(2,1)S(1)}, u32[]{:S(2)}, u32[]{:S(2)}) async-start(bf16[8,32,768]{2,1,0:T(8,128)(2,1)} %bitcast.2), calls=%async_computation | async-start | bytes 786432 | tf_op jit(solution)/shard_map/all_to_all | solution.py:32
  20.9 303.7 %reduce-scatter.2.cloned.1.call-start = ((), (), s32[]{:S(2)}) async-start(), calls=%async_computation.7 | async-start | bytes 3170304 | tf_op jit(solution)/shard_map/reduce_scatter | solution.py:72
  120.1 21.5 %all-to-all-start.3 = ((bf16[8,32,768]{2,1,0:T(8,128)(2,1)}), bf16[8,32,768]{2,1,0:T(8,128)(2,1)S(1)}, u32[]{:S(2)}, u32[]{:S(2)}) async-start(bf16[8,32,768]{2,1,0:T(8,128)(2,1)} %bitcast.8), calls=%async_computation.3 | async-start | bytes 786432 | tf_op jit(solution)/shard_map/all_to_all | solution.py:48
  141.7 185.3 %all-to-all-start.1 = ((bf16[8,32,1024]{2,1,0:T(8,128)(2,1)}), bf16[8,32,1024]{2,1,0:T(8,128)(2,1)S(1)}, u32[]{:S(2)}, u32[]{:S(2)}) async-start(bf16[8,32,1024]{2,1,0:T(8,128)(2,1)} %bitcast.4), calls=%async_computation.1 | async-start | bytes 1048576 | tf_op jit(solution)/shard_map/all_to_all | solution.py:34
  326.9 33.8 %all-to-all-start.4 = ((f32[128,6,8]{1,2,0:T(8,128)}), f32[128,6,8]{1,2,0:T(8,128)S(1)}, u32[]{:S(2)}, u32[]{:S(2)}) async-start(f32[128,6,8]{1,2,0:T(8,128)} %copy.16), calls=%async_computation.5 | async-start | bytes 1048576 | tf_op jit(solution)/shard_map/all_to_all | solution.py:73
Sparse Core Ops, SparseCore 0:
  12.9 103.8 all-gather.1
  122.3 202.2 reduce-scatter.1
where the time goes:
time: 369 us; the launch traced here: 368 us
  waiting for transfers between devices  286 us (78%)
  starting transfers between devices  31.6 us (9%)
  blocking collectives  16.3 us (4%)
  between operations  14.8 us (4%)
  matrix products  13.2 us (4%)
  local copies, waits for them, and re-layouts  4.49 us (1%)
    reduce_scatter x1, waiting for transfers between devices, on_device(): lax.psum_scatter(partial_grad, 'dp', scatter_dimension=1, tiled=True)  179 us
    all_gather x1, waiting for transfers between devices, on_device(): weight = lax.all_gather(down_weight, 'dp', axis=1, tiled=True)[0]  66.5 us
    all_to_all x1, waiting for transfers between devices, on_device(): lax.all_to_all(summed, 'dp', split_axis=0, concat_axis=1, tiled=True)  18.5 us
    all_to_all x1, blocking collectives, on_device(): lax.all_to_all(g_send, 'expert', split_axis=0, concat_axis=0, tiled=True)  16.3 us
    all_to_all x1, starting transfers between devices, on_device(): lax.all_to_all(summed, 'dp', split_axis=0, concat_axis=1, tiled=True)  14.3 us
    all_to_all x1, waiting for transfers between devices, on_device(): lax.all_to_all(result.astype(jnp.bfloat16).reshape(groups, CAP, -1), 'exp...  11.8 us
    all_to_all x1, waiting for transfers between devices, on_device(): lax.all_to_all(h_send, 'expert', split_axis=0, concat_axis=0, tiled=True)  10.4 us
  transfers between devices with their start and end apart: 6, of which 5 were waited for; matrix products, arithmetic and copies ran while one was open for 5% of the time, Pallas kernels for 0%

commit v1 on v0

v1 whole, which is shorter than its diff:
```python
import jax
import jax.numpy as jnp
from jax import lax
from jax.sharding import Mesh
from jax.sharding import PartitionSpec as P

CAP = 32
DP = ("y", "z", "c")


def on_device(hidden, cotangent, expert_ids, counts, down_weight):
    tok_rows, ff = hidden.shape
    d = cotangent.shape[1]
    groups = lax.axis_size("expert")
    ny, nz, nc = lax.axis_size("y"), lax.axis_size("z"), lax.axis_size("c")
    width = groups * CAP
    ids = expert_ids[:, 0]
    live = jnp.arange(tok_rows, dtype=jnp.int32) < counts[0, 0]
    member = (ids[:, None] == jnp.arange(groups, dtype=jnp.int32)[None, :]).astype(jnp.int32)
    rank = jnp.sum((jnp.cumsum(member, 0) - 1) * member, 1)
    target = ids * CAP + rank
    placing = jnp.logical_and(
        target[None, :] == jnp.arange(width, dtype=jnp.int32)[:, None], live[None, :]
    ).astype(jnp.bfloat16)
    both = jnp.concatenate([hidden, cotangent], axis=1)
    send = (
        jnp.dot(placing, both, preferred_element_type=jnp.float32)
        .astype(jnp.bfloat16)
        .reshape(groups, CAP, ff + d)
    )
    weight = lax.all_gather(down_weight, DP, axis=1, tiled=True)[0]
    recv = lax.all_to_all(send, "expert", split_axis=0, concat_axis=0, tiled=True).reshape(width, ff + d)
    h_rows = recv[:, :ff]
    g_rows = recv[:, ff:]
    rows_dev = ff // (ny * nz * nc)
    h_perm = h_rows.reshape(width, ny, nz, nc, rows_dev).transpose(0, 3, 2, 1, 4).reshape(width, ff)
    partial_grad = lax.dot_general(
        h_perm, g_rows, (((0,), (0,)), ((), ())), preferred_element_type=jnp.float32
    )
    summed = partial_grad
    for axis, n in (("c", nc), ("z", nz), ("y", ny)):
        parts = lax.all_to_all(
            summed.reshape(n, summed.shape[0] // n, d), axis, split_axis=0, concat_axis=0, tiled=True
        )
        summed = jnp.sum(parts, axis=0)
    y_rows = jnp.dot(h_rows, weight, preferred_element_type=jnp.float32).astype(jnp.bfloat16)
    dh_rows = lax.dot_general(
        g_rows, weight, (((1,), (1,)), ((), ())), preferred_element_type=jnp.float32
    ).astype(jnp.bfloat16)
    back = lax.all_to_all(
        jnp.concatenate([y_rows, dh_rows], axis=1).reshape(groups, CAP, d + ff),
        "expert",
        split_axis=0,
        concat_axis=0,
        tiled=True,
    ).reshape(width, d + ff)
    output = lax.dot_general(
        placing, back[:, :d], (((0,), (0,)), ((), ())), preferred_element_type=jnp.float32
    ).astype(jnp.bfloat16)
    hidden_grad = lax.dot_general(
        placing, back[:, d:], (((0,), (0,)), ((), ())), preferred_element_type=jnp.float32
    ).astype(jnp.bfloat16)
    return (output, hidden_grad, summed[None])


def solution(mesh):
    ex, dp = mesh.devices.shape
    view = Mesh(mesh.devices.reshape(ex, dp // 16, 8, 2), ("expert",) + DP)
    tokens = P(("expert",) + DP, None)
    placed = (tokens, tokens, tokens, P("expert", DP), P("expert", DP, None))
    return jax.shard_map(
        on_device,
        mesh=view,
        in_specs=placed,
        out_specs=(tokens, tokens, P("expert", DP, None)),
        check_vma=False,
    )
```

time: 369 us -> 197 us (0.53)
  waiting for transfers between devices: 286 us -> 114 us
    reduce_scatter x1 -> x0, waiting for transfers between devices: 179 us -> none  [on_device(): lax.psum_scatter(partial_grad, 'dp', scatter_dimension=1, tiled=True)]
    all_to_all x4, waiting for transfers between devices: 40.6 us -> 49.9 us  [the longest x1 25.7 us: on_device(): lax.all_to_all(jnp.concatenate([y_rows, dh_rows], axis=1).reshape(groups,...]
    dot_general x7 -> x6, matrix products: 13.2 us -> 9.95 us  [the longest x1 2.59 us: on_device(): lax.dot_general(g_rows, weight, (((1,), (1,)), ((), ())), preferred_eleme...]
  transfers between devices with their start and end apart: 6 -> 5, of which waited for: 5 -> 4; matrix products, arithmetic and copies ran while one was open for 5% -> 5% of each run, Pallas kernels for 0% -> 0%
where the time goes in v1:
time: 197 us
  waiting for transfers between devices  114 us (58%)
  starting transfers between devices  32.8 us (17%)
  blocking collectives  17.2 us (9%)
  between operations  14.8 us (8%)
  matrix products  9.95 us (5%)
  other arithmetic  5.12 us (3%)
  local copies, waits for them, and re-layouts  2.9 us (1%)
    all_gather x1, waiting for transfers between devices, on_device(): weight = lax.all_gather(down_weight, DP, axis=1, tiled=True)[0]  64 us
    all_to_all x1, waiting for transfers between devices, on_device(): lax.all_to_all(jnp.concatenate([y_rows, dh_rows], axis=1).reshape(groups,...  25.7 us
    all_to_all x2, starting transfers between devices, on_device(): lax.all_to_all(summed.reshape(n, summed.shape[0] // n, d), axis, split_ax...  20.5 us
    all_to_all x1, blocking collectives, on_device(): lax.all_to_all(summed.reshape(n, summed.shape[0] // n, d), axis, split_ax...  17.2 us
    all_to_all x1, waiting for transfers between devices, on_device(): lax.all_to_all(send, 'expert', split_axis=0, concat_axis=0, tiled=True)  15.8 us
    all_to_all x2, waiting for transfers between devices, on_device(): lax.all_to_all(summed.reshape(n, summed.shape[0] // n, d), axis, split_ax...  8.35 us
    all_to_all x1, starting transfers between devices, on_device(): lax.all_to_all(send, 'expert', split_axis=0, concat_axis=0, tiled=True)  7.31 us
    all_to_all x1, starting transfers between devices, on_device(): lax.all_to_all(jnp.concatenate([y_rows, dh_rows], axis=1).reshape(groups,...  5 us
  transfers between devices with their start and end apart: 5, of which 4 were waited for; matrix products, arithmetic and copies ran while one was open for 5% of the time, Pallas kernels for 0%

profile of v1, /device:TPU:1, one launch (start us, length us, event | category | flops | bytes accessed | tf_op | source)
XLA Modules:
  0.0 196.7 jit_solution(10813409359198148578)
XLA Ops:
  7.8 0.7 fusion.28
  8.6 0.2 reduce_window_sum.11
  8.8 0.8 select_reduce_fusion
  9.6 0.7 multiply_add_fusion
  10.3 2.3 %convolution_convert_fusion = bf16[256,1792]{1,0:T(8,128)(2,1)} fusion(bf16[128,1024]{1,0:T(8,128)(2,1)} %param.6, bf16[128,768]{1,0:T(8,128)(2,1)} %param.5, s32[128]{0:T(128)S(1)} %multiply_add_fusion, pred[128]{0:T(512)(128)(4,1)S(1)} %iota_compare_fusion.2), kind=kOutput, calls=%fused_computation | convolution fusion | flops 118882304 | bytes 1376896 | tf_op jit(solution)/shard_map/dot_general | solution.py:27
  12.6 7.3 %all-to-all-start = ((bf16[8,32,1792]{2,1,0:T(8,128)(2,1)}), bf16[8,32,1792]{2,1,0:T(8,128)(2,1)S(1)}, u32[]{:S(2)}, u32[]{:S(2)}) async-start(bf16[8,32,1792]{2,1,0:T(8,128)(2,1)} %bitcast.2), calls=%async_computation | async-start | bytes 1835008 | tf_op jit(solution)/shard_map/all_to_all | solution.py:32
  19.9 0.0 all-gather.2.cloned.1.call-start
  19.9 0.6 copy.16
  20.6 0.0 all-gather.2.cloned.1.call-update
  20.6 15.8 %all-to-all-done = bf16[8,32,1792]{2,1,0:T(8,128)(2,1)S(1)} async-done(((bf16[8,32,1792]{2,1,0:T(8,128)(2,1)}), bf16[8,32,1792]{2,1,0:T(8,128)(2,1)S(1)}, u32[]{:S(2)}, u32[]{:S(2)}) %all-to-all-start) | async-done | bytes 917536 | tf_op jit(solution)/shard_map/all_to_all | solution.py:32
  36.4 0.2 copy.17
  36.6 0.1 reshape.48
  36.8 0.1 reshape.49
  36.9 0.4 copy-done
  37.3 0.6 fusion.13
  37.9 17.2 %all_to_all.25 = f32[2,384,1024]{2,1,0:T(8,128)S(1)} all-to-all(f32[2,384,1024]{2,1,0:T(8,128)S(1)} %fusion.13), channel_id=1, replica_groups=mesh['expert'=8,'y'=8,'z'=8,'c'=2] {'c'}, dimensions={0} | all-to-all | bytes 6291456 | tf_op jit(solution)/shard_map/all_to_all | solution.py:42
  55.1 1.6 reduce_sum.37
  56.7 15.6 %all-to-all-start.3 = ((f32[8,48,1024]{2,1,0:T(8,128)}), f32[8,48,1024]{2,1,0:T(8,128)S(1)}, u32[]{:S(2)}, u32[]{:S(2)}) async-start(f32[8,48,1024]{2,1,0:T(8,128)} %bitcast.30), calls=%async_computation.3 | async-start | bytes 3145728 | tf_op jit(solution)/shard_map/all_to_all | solution.py:42
  72.3 64.0 %all-gather.2.cloned.1.call-done = bf16[1,768,1024]{2,0,1:T(2,128)(2,1)} async-done(((bf16[1,6,1024]{2,0,1:T(2,128)(2,1)}), bf16[1,768,1024]{2,0,1:T(2,128)(2,1)}) %all-gather.2.cloned.1.call-update) | async-done | bytes 1572880 | tf_op jit(solution)/shard_map/all_gather | solution.py:31
  136.3 2.6 %fusion.7 = bf16[256,768]{1,0:T(8,128)(2,1)S(1)} fusion(bf16[1,768,1024]{2,0,1:T(2,128)(2,1)} %all-gather.2.cloned.1.call-done, bf16[256,1792]{1,0:T(8,128)(2,1)S(1)} %bitcast.35), kind=kOutput, calls=%fused_computation.6 | convolution fusion | flops 402849792 | bytes 2490368 | tf_op jit(solution)/shard_map/dot_general | solution.py:47
  138.9 0.0 all-to-all-done.3
  138.9 0.1 reduce_sum.38
  139.0 0.7 reshape.51
  139.7 4.9 %all-to-all-start.4 = ((f32[8,6,1024]{2,1,0:T(8,128)}), f32[8,6,1024]{2,1,0:T(8,128)S(1)}, u32[]{:S(2)}, u32[]{:S(2)}) async-start(f32[8,6,1024]{2,1,0:T(8,128)} %reshape.51), calls=%async_computation.4 | async-start | bytes 524288 | tf_op jit(solution)/shard_map/all_to_all | solution.py:42
  144.6 2.6 %fusion.4 = bf16[256,1024]{1,0:T(8,128)(2,1)S(1)} fusion(bf16[1,768,1024]{2,0,1:T(2,128)(2,1)} %all-gather.2.cloned.1.call-done, bf16[256,1792]{1,0:T(8,128)(2,1)S(1)} %bitcast.36), kind=kOutput, calls=%fused_computation.5 | convolution fusion | flops 402915328 | bytes 2490368 | tf_op jit(solution)/shard_map/dot_general | solution.py:46
  147.2 1.0 pad_maximum_fusion
  148.2 8.3 %all-to-all-done.4 = f32[8,6,1024]{2,1,0:T(8,128)S(1)} async-done(((f32[8,6,1024]{2,1,0:T(8,128)}), f32[8,6,1024]{2,1,0:T(8,128)S(1)}, u32[]{:S(2)}, u32[]{:S(2)}) %all-to-all-start.4) | async-done | bytes 196640 | tf_op jit(solution)/shard_map/all_to_all | solution.py:42
  156.5 5.0 %all-to-all-start.1 = ((bf16[8,32,1792]{2,1,0:T(8,128)(2,1)}), bf16[8,32,1792]{2,1,0:T(8,128)(2,1)S(1)}, u32[]{:S(2)}, u32[]{:S(2)}) async-start(bf16[8,32,1792]{2,1,0:T(8,128)(2,1)} %bitcast.4), calls=%async_computation.1 | async-start | bytes 1835008 | tf_op jit(solution)/shard_map/all_to_all | solution.py:50
  161.5 0.6 broadcast_in_dim.2
  162.2 25.7 %all-to-all-done.1 = bf16[8,32,1792]{2,1,0:T(8,128)(2,1)S(1)} async-done(((bf16[8,32,1792]{2,1,0:T(8,128)(2,1)}), bf16[8,32,1792]{2,1,0:T(8,128)(2,1)S(1)}, u32[]{:S(2)}, u32[]{:S(2)}) %all-to-all-start.1) | async-done | bytes 917536 | tf_op jit(solution)/shard_map/all_to_all | solution.py:50
  187.9 0.9 convolution_convert_fusion.2
  188.8 1.0 convolution_convert_fusion.1
  (9 shorter events, 0.1 us)
Async XLA Ops:
  7.2 12.8 %copy-start.2 = (bf16[1,6,1024]{2,1,0:T(8,128)(2,1)S(1)}, bf16[1,6,1024]{2,1,0:T(8,128)(2,1)}, u32[]{:S(2)}) copy-start(bf16[1,6,1024]{2,1,0:T(8,128)(2,1)} %param.9) | copy-start | bytes 36868
  12.6 23.8 %all-to-all-start = ((bf16[8,32,1792]{2,1,0:T(8,128)(2,1)}), bf16[8,32,1792]{2,1,0:T(8,128)(2,1)S(1)}, u32[]{:S(2)}, u32[]{:S(2)}) async-start(bf16[8,32,1792]{2,1,0:T(8,128)(2,1)} %bitcast.2), calls=%async_computation | async-start | bytes 1835008 | tf_op jit(solution)/shard_map/all_to_all | solution.py:32
  19.9 116.4 %all-gather.2.cloned.1.call-start = ((), (), s32[]{:S(2)}) async-start(), calls=%async_computation.5 | async-start | bytes 3170304 | tf_op jit(solution)/shard_map/all_gather | solution.py:31
  36.4 0.9 copy-start
  56.7 79.6 %copy-start.1 = (bf16[8,32,1792]{2,1,0:T(8,128)(2,1)S(1)}, bf16[8,32,1792]{2,1,0:T(8,128)(2,1)}, u32[]{:S(2)}) copy-start(bf16[8,32,1792]{2,1,0:T(8,128)(2,1)} %copy-done) | copy-start | bytes 2752516
  56.7 82.2 %all-to-all-start.3 = ((f32[8,48,1024]{2,1,0:T(8,128)}), f32[8,48,1024]{2,1,0:T(8,128)S(1)}, u32[]{:S(2)}, u32[]{:S(2)}) async-start(f32[8,48,1024]{2,1,0:T(8,128)} %bitcast.30), calls=%async_computation.3 | async-start | bytes 3145728 | tf_op jit(solution)/shard_map/all_to_all | solution.py:42
  139.7 16.8 %all-to-all-start.4 = ((f32[8,6,1024]{2,1,0:T(8,128)}), f32[8,6,1024]{2,1,0:T(8,128)S(1)}, u32[]{:S(2)}, u32[]{:S(2)}) async-start(f32[8,6,1024]{2,1,0:T(8,128)} %reshape.51), calls=%async_computation.4 | async-start | bytes 524288 | tf_op jit(solution)/shard_map/all_to_all | solution.py:42
  156.5 31.4 %all-to-all-start.1 = ((bf16[8,32,1792]{2,1,0:T(8,128)(2,1)}), bf16[8,32,1792]{2,1,0:T(8,128)(2,1)S(1)}, u32[]{:S(2)}, u32[]{:S(2)}) async-start(bf16[8,32,1792]{2,1,0:T(8,128)(2,1)} %bitcast.4), calls=%async_computation.1 | async-start | bytes 1835008 | tf_op jit(solution)/shard_map/all_to_all | solution.py:50
Sparse Core Ops, SparseCore 0:
  25.6 110.6 all-gather.1

commit v2 on v1

--- a/solution.py
+++ b/solution.py
@@ -28,7 +28,11 @@
         .astype(jnp.bfloat16)
         .reshape(groups, CAP, ff + d)
     )
-    weight = lax.all_gather(down_weight, DP, axis=1, tiled=True)[0]
+    weight = down_weight[0]
+    for axis, n in (("c", nc), ("z", nz), ("y", ny)):
+        weight = lax.all_to_all(
+            jnp.broadcast_to(weight, (n,) + weight.shape), axis, split_axis=0, concat_axis=0, tiled=True
+        ).reshape(n * weight.shape[0], d)
     recv = lax.all_to_all(send, "expert", split_axis=0, concat_axis=0, tiled=True).reshape(width, ff + d)
     h_rows = recv[:, :ff]
     g_rows = recv[:, ff:]

time: 197 us -> 211 us (1.071); the launches traced: 197 us -> 207 us
  waiting for transfers between devices: 114 us -> 135 us
  between operations: 14.8 us -> 1.41 us
  blocking collectives: 17.2 us -> 23.9 us
  starting transfers between devices: 32.8 us -> 28.2 us
  local copies, waits for them, and re-layouts: 2.9 us -> 5.1 us
    all_gather x1 -> x0, waiting for transfers between devices: 64 us -> none  [on_device(): weight = lax.all_gather(down_weight, DP, axis=1, tiled=True)[0]]
    all_to_all x0 -> x2, waiting for transfers between devices: none -> 42.6 us  [on_device(): lax.all_to_all(jnp.broadcast_to(weight, (n,) + weight.shape), axis, split...]
    all_to_all x2, waiting for transfers between devices: 8.35 us -> 42.7 us  [on_device(): lax.all_to_all(summed.reshape(n, summed.shape[0] // n, d), axis, split_ax...]
    all_to_all x0 -> x1, blocking collectives: none -> 17.5 us  [on_device(): lax.all_to_all(jnp.broadcast_to(weight, (n,) + weight.shape), axis, split...]
    all_to_all x2, starting transfers between devices: 20.5 us -> 7.12 us  [on_device(): lax.all_to_all(summed.reshape(n, summed.shape[0] // n, d), axis, split_ax...]
    all_to_all x0 -> x2, starting transfers between devices: none -> 11 us  [on_device(): lax.all_to_all(jnp.broadcast_to(weight, (n,) + weight.shape), axis, split...]
    all_to_all x1, blocking collectives: 17.2 us -> 6.38 us  [on_device(): lax.all_to_all(summed.reshape(n, summed.shape[0] // n, d), axis, split_ax...]
    all_to_all x1, waiting for transfers between devices: 15.8 us -> 26.3 us  [on_device(): lax.all_to_all(send, 'expert', split_axis=0, concat_axis=0, tiled=True)]
  transfers between devices with their start and end apart: 5 -> 6, of which waited for: 4 -> 6; matrix products, arithmetic and copies ran while one was open for 5% -> 7% of each run, Pallas kernels for 0% -> 0%
where the time goes in v2:
time: 211 us; the launch traced here: 207 us
  waiting for transfers between devices  135 us (64%)
  starting transfers between devices  28.2 us (13%)
  blocking collectives  23.9 us (11%)
  matrix products  8.81 us (4%)
  local copies, waits for them, and re-layouts  5.1 us (2%)
  other arithmetic  5.07 us (2%)
    all_to_all x2, waiting for transfers between devices, on_device(): lax.all_to_all(summed.reshape(n, summed.shape[0] // n, d), axis, split_ax...  42.7 us
    all_to_all x2, waiting for transfers between devices, on_device(): lax.all_to_all(jnp.broadcast_to(weight, (n,) + weight.shape), axis, split...  42.6 us
    all_to_all x1, waiting for transfers between devices, on_device(): lax.all_to_all(send, 'expert', split_axis=0, concat_axis=0, tiled=True)  26.3 us
    all_to_all x1, waiting for transfers between devices, on_device(): lax.all_to_all(jnp.concatenate([y_rows, dh_rows], axis=1).reshape(groups,...  23.3 us
    all_to_all x1, blocking collectives, on_device(): lax.all_to_all(jnp.broadcast_to(weight, (n,) + weight.shape), axis, split...  17.5 us
    all_to_all x2, starting transfers between devices, on_device(): lax.all_to_all(jnp.broadcast_to(weight, (n,) + weight.shape), axis, split...  11 us
    all_to_all x2, starting transfers between devices, on_device(): lax.all_to_all(summed.reshape(n, summed.shape[0] // n, d), axis, split_ax...  7.12 us
    all_to_all x1, starting transfers between devices, on_device(): lax.all_to_all(send, 'expert', split_axis=0, concat_axis=0, tiled=True)  6.48 us
  transfers between devices with their start and end apart: 6, of which 6 were waited for; matrix products, arithmetic and copies ran while one was open for 7% of the time, Pallas kernels for 0%

profile of v2, /device:TPU:1, one launch (start us, length us, event | category | flops | bytes accessed | tf_op | source)
XLA Modules:
  0.0 207.4 jit_solution(14728764029785584421)
XLA Ops:
  0.6 0.7 broadcast_in_dim.16
  1.4 17.5 %all_to_all.40 = bf16[2,6,1024]{2,1,0:T(8,128)(2,1)S(1)} all-to-all(bf16[2,6,1024]{2,1,0:T(8,128)(2,1)S(1)} %broadcast_in_dim.16), channel_id=1, replica_groups=mesh['expert'=8,'y'=8,'z'=8,'c'=2] {'c'}, dimensions={0} | all-to-all | bytes 49152 | tf_op jit(solution)/shard_map/all_to_all | solution.py:33
  18.9 0.7 broadcast_in_dim.17
  19.6 3.8 %all-to-all-start.2 = ((bf16[8,12,1024]{2,1,0:T(8,128)(2,1)}), bf16[8,12,1024]{2,1,0:T(8,128)(2,1)S(1)}, u32[]{:S(2)}, u32[]{:S(2)}) async-start(bf16[8,12,1024]{2,1,0:T(8,128)(2,1)} %broadcast_in_dim.17), calls=%async_computation.2 | async-start | bytes 524288 | tf_op jit(solution)/shard_map/all_to_all | solution.py:33
  24.0 0.7 fusion.16
  24.8 0.2 reduce_window_sum.11
  25.0 0.8 select_reduce_fusion
  25.8 0.7 multiply_add_fusion
  26.5 2.3 %convolution_convert_fusion = bf16[256,1792]{1,0:T(8,128)(2,1)} fusion(bf16[128,1024]{1,0:T(8,128)(2,1)} %param.6, bf16[128,768]{1,0:T(8,128)(2,1)} %param.5, s32[128]{0:T(128)S(1)} %multiply_add_fusion, pred[128]{0:T(512)(128)(4,1)S(1)} %iota_compare_fusion.2), kind=kOutput, calls=%fused_computation | convolution fusion | flops 118882304 | bytes 1376896 | tf_op jit(solution)/shard_map/dot_general | solution.py:27
  28.8 5.8 %all-to-all-done.2 = bf16[8,12,1024]{2,1,0:T(8,128)(2,1)S(1)} async-done(((bf16[8,12,1024]{2,1,0:T(8,128)(2,1)}), bf16[8,12,1024]{2,1,0:T(8,128)(2,1)S(1)}, u32[]{:S(2)}, u32[]{:S(2)}) %all-to-all-start.2) | async-done | bytes 196640 | tf_op jit(solution)/shard_map/all_to_all | solution.py:33
  34.6 6.5 %all-to-all-start = ((bf16[8,32,1792]{2,1,0:T(8,128)(2,1)}), bf16[8,32,1792]{2,1,0:T(8,128)(2,1)S(1)}, u32[]{:S(2)}, u32[]{:S(2)}) async-start(bf16[8,32,1792]{2,1,0:T(8,128)(2,1)} %bitcast.2), calls=%async_computation | async-start | bytes 1835008 | tf_op jit(solution)/shard_map/all_to_all | solution.py:36
  41.1 26.3 %all-to-all-done = bf16[8,32,1792]{2,1,0:T(8,128)(2,1)S(1)} async-done(((bf16[8,32,1792]{2,1,0:T(8,128)(2,1)}), bf16[8,32,1792]{2,1,0:T(8,128)(2,1)S(1)}, u32[]{:S(2)}, u32[]{:S(2)}) %all-to-all-start) | async-done | bytes 917536 | tf_op jit(solution)/shard_map/all_to_all | solution.py:36
  68.0 0.4 copy-done
  68.4 0.6 fusion.1
  69.0 6.4 %all_to_all.41 = f32[2,384,1024]{2,1,0:T(8,128)S(1)} all-to-all(f32[2,384,1024]{2,1,0:T(8,128)S(1)} %fusion.1), channel_id=1, replica_groups=mesh['expert'=8,'y'=8,'z'=8,'c'=2] {'c'}, dimensions={0} | all-to-all | bytes 6291456 | tf_op jit(solution)/shard_map/all_to_all | solution.py:46
  75.4 1.3 broadcast_in_dim.18
  76.7 7.3 %all-to-all-start.3 = ((bf16[8,96,1024]{2,1,0:T(8,128)(2,1)}), bf16[8,96,1024]{2,1,0:T(8,128)(2,1)}, u32[]{:S(2)}, u32[]{:S(2)}) async-start(bf16[8,96,1024]{2,1,0:T(8,128)(2,1)} %broadcast_in_dim.18), calls=%async_computation.3 | async-start | bytes 3145728 | tf_op jit(solution)/shard_map/all_to_all | solution.py:33
  84.0 1.6 reduce_sum.37
  85.5 36.8 %all-to-all-done.3 = bf16[8,96,1024]{2,1,0:T(8,128)(2,1)} async-done(((bf16[8,96,1024]{2,1,0:T(8,128)(2,1)}), bf16[8,96,1024]{2,1,0:T(8,128)(2,1)}, u32[]{:S(2)}, u32[]{:S(2)}) %all-to-all-start.3) | async-done | bytes 1572896 | tf_op jit(solution)/shard_map/all_to_all | solution.py:33
  122.3 3.7 %all-to-all-start.6 = ((f32[8,48,1024]{2,1,0:T(8,128)}), f32[8,48,1024]{2,1,0:T(8,128)S(1)}, u32[]{:S(2)}, u32[]{:S(2)}) async-start(f32[8,48,1024]{2,1,0:T(8,128)} %bitcast.25), calls=%async_computation.6 | async-start | bytes 3145728 | tf_op jit(solution)/shard_map/all_to_all | solution.py:46
  126.1 2.0 convolution_convert_fusion.2
  128.1 2.0 convolution_convert_fusion.1
  130.1 1.0 pad_maximum_fusion
  131.1 35.3 %all-to-all-done.6 = f32[8,48,1024]{2,1,0:T(8,128)S(1)} async-done(((f32[8,48,1024]{2,1,0:T(8,128)}), f32[8,48,1024]{2,1,0:T(8,128)S(1)}, u32[]{:S(2)}, u32[]{:S(2)}) %all-to-all-start.6) | async-done | bytes 1572896 | tf_op jit(solution)/shard_map/all_to_all | solution.py:46
  166.4 3.6 %all-to-all-start.4 = ((bf16[8,32,1792]{2,1,0:T(8,128)(2,1)}), bf16[8,32,1792]{2,1,0:T(8,128)(2,1)S(1)}, u32[]{:S(2)}, u32[]{:S(2)}) async-start(bf16[8,32,1792]{2,1,0:T(8,128)(2,1)} %bitcast.6), calls=%async_computation.4 | async-start | bytes 1835008 | tf_op jit(solution)/shard_map/all_to_all | solution.py:54
  170.1 0.7 reshape.63
  170.8 23.3 %all-to-all-done.4 = bf16[8,32,1792]{2,1,0:T(8,128)(2,1)S(1)} async-done(((bf16[8,32,1792]{2,1,0:T(8,128)(2,1)}), bf16[8,32,1792]{2,1,0:T(8,128)(2,1)S(1)}, u32[]{:S(2)}, u32[]{:S(2)}) %all-to-all-start.4) | async-done | bytes 917536 | tf_op jit(solution)/shard_map/all_to_all | solution.py:54
  194.1 3.4 %all-to-all-start.7 = ((f32[8,6,1024]{2,1,0:T(8,128)}), f32[8,6,1024]{2,1,0:T(8,128)S(1)}, u32[]{:S(2)}, u32[]{:S(2)}) async-start(f32[8,6,1024]{2,1,0:T(8,128)} %reshape.63), calls=%async_computation.7 | async-start | bytes 524288 | tf_op jit(solution)/shard_map/all_to_all | solution.py:46
  197.5 0.9 convolution_convert_fusion.4
  198.4 1.0 convolution_convert_fusion.3
  199.4 7.4 %all-to-all-done.7 = f32[8,6,1024]{2,1,0:T(8,128)S(1)} async-done(((f32[8,6,1024]{2,1,0:T(8,128)}), f32[8,6,1024]{2,1,0:T(8,128)S(1)}, u32[]{:S(2)}, u32[]{:S(2)}) %all-to-all-start.7) | async-done | bytes 196640 | tf_op jit(solution)/shard_map/all_to_all | solution.py:46
  206.8 0.6 broadcast_in_dim.19
  (13 shorter events, 0.7 us)
Async XLA Ops:
  19.6 15.0 %all-to-all-start.2 = ((bf16[8,12,1024]{2,1,0:T(8,128)(2,1)}), bf16[8,12,1024]{2,1,0:T(8,128)(2,1)S(1)}, u32[]{:S(2)}, u32[]{:S(2)}) async-start(bf16[8,12,1024]{2,1,0:T(8,128)(2,1)} %broadcast_in_dim.17), calls=%async_computation.2 | async-start | bytes 524288 | tf_op jit(solution)/shard_map/all_to_all | solution.py:33
  34.6 32.9 %all-to-all-start = ((bf16[8,32,1792]{2,1,0:T(8,128)(2,1)}), bf16[8,32,1792]{2,1,0:T(8,128)(2,1)S(1)}, u32[]{:S(2)}, u32[]{:S(2)}) async-start(bf16[8,32,1792]{2,1,0:T(8,128)(2,1)} %bitcast.2), calls=%async_computation | async-start | bytes 1835008 | tf_op jit(solution)/shard_map/all_to_all | solution.py:36
  67.5 0.9 copy-start
  76.7 45.6 %all-to-all-start.3 = ((bf16[8,96,1024]{2,1,0:T(8,128)(2,1)}), bf16[8,96,1024]{2,1,0:T(8,128)(2,1)}, u32[]{:S(2)}, u32[]{:S(2)}) async-start(bf16[8,96,1024]{2,1,0:T(8,128)(2,1)} %broadcast_in_dim.18), calls=%async_computation.3 | async-start | bytes 3145728 | tf_op jit(solution)/shard_map/all_to_all | solution.py:33
  122.3 3.7 %copy-start.1 = (bf16[8,32,1792]{2,1,0:T(8,128)(2,1)S(1)}, bf16[8,32,1792]{2,1,0:T(8,128)(2,1)}, u32[]{:S(2)}) copy-start(bf16[8,32,1792]{2,1,0:T(8,128)(2,1)} %copy-done) | copy-start | bytes 2752516
  122.3 44.1 %all-to-all-start.6 = ((f32[8,48,1024]{2,1,0:T(8,128)}), f32[8,48,1024]{2,1,0:T(8,128)S(1)}, u32[]{:S(2)}, u32[]{:S(2)}) async-start(f32[8,48,1024]{2,1,0:T(8,128)} %bitcast.25), calls=%async_computation.6 | async-start | bytes 3145728 | tf_op jit(solution)/shard_map/all_to_all | solution.py:46
  166.4 27.6 %all-to-all-start.4 = ((bf16[8,32,1792]{2,1,0:T(8,128)(2,1)}), bf16[8,32,1792]{2,1,0:T(8,128)(2,1)S(1)}, u32[]{:S(2)}, u32[]{:S(2)}) async-start(bf16[8,32,1792]{2,1,0:T(8,128)(2,1)} %bitcast.6), calls=%async_computation.4 | async-start | bytes 1835008 | tf_op jit(solution)/shard_map/all_to_all | solution.py:54
  194.1 12.7 %all-to-all-start.7 = ((f32[8,6,1024]{2,1,0:T(8,128)}), f32[8,6,1024]{2,1,0:T(8,128)S(1)}, u32[]{:S(2)}, u32[]{:S(2)}) async-start(f32[8,6,1024]{2,1,0:T(8,128)} %reshape.63), calls=%async_computation.7 | async-start | bytes 524288 | tf_op jit(solution)/shard_map/all_to_all | solution.py:46

commit v3 on v1

--- a/solution.py
+++ b/solution.py
@@ -43,6 +43,7 @@
             summed.reshape(n, summed.shape[0] // n, d), axis, split_axis=0, concat_axis=0, tiled=True
         )
         summed = jnp.sum(parts, axis=0)
+    summed, weight = lax.optimization_barrier((summed, weight))
     y_rows = jnp.dot(h_rows, weight, preferred_element_type=jnp.float32).astype(jnp.bfloat16)
     dh_rows = lax.dot_general(
         g_rows, weight, (((1,), (1,)), ((), ())), preferred_element_type=jnp.float32

time: 197 us -> 179 us (0.909)
  waiting for transfers between devices: 114 us -> 53.5 us
  blocking collectives: 17.2 us -> 74.4 us
  starting transfers between devices: 32.8 us -> 19.9 us
  matrix products: 9.95 us -> 5.99 us
  local copies, waits for them, and re-layouts: 2.9 us -> 5.38 us
    all_to_all x1 -> x2, blocking collectives: 17.2 us -> 74.4 us  [on_device(): lax.all_to_all(summed.reshape(n, summed.shape[0] // n, d), axis, split_ax...]
    all_gather x1, waiting for transfers between devices: 64 us -> 11.9 us  [on_device(): weight = lax.all_gather(down_weight, DP, axis=1, tiled=True)[0]]
    all_to_all x2 -> x1, starting transfers between devices: 20.5 us -> 7.63 us  [on_device(): lax.all_to_all(summed.reshape(n, summed.shape[0] // n, d), axis, split_ax...]
    all_to_all x2 -> x1, waiting for transfers between devices: 8.35 us -> 0.01 us  [on_device(): lax.all_to_all(summed.reshape(n, summed.shape[0] // n, d), axis, split_ax...]
    unnamed x7 -> x8, local copies, waits for them, and re-layouts: 1.04 us -> 3.52 us
    dot_general x1, matrix products: 2.56 us -> 0.58 us  [on_device(): jnp.dot(h_rows, weight, preferred_element_type=jnp.float32)]
    dot_general x1, matrix products: 2.59 us -> 0.61 us  [on_device(): lax.dot_general(g_rows, weight, (((1,), (1,)), ((), ())), preferred_eleme...]
  transfers between devices with their start and end apart: 5 -> 4, of which waited for: 4 -> 3; matrix products, arithmetic and copies ran while one was open for 5% -> 4% of each run, Pallas kernels for 0% -> 0%
where the time goes in v3:
time: 179 us
  blocking collectives  74.4 us (42%)
  waiting for transfers between devices  53.5 us (30%)
  starting transfers between devices  19.9 us (11%)
  between operations  14.8 us (8%)
  matrix products  5.99 us (3%)
  local copies, waits for them, and re-layouts  5.38 us (3%)
  other arithmetic  5.05 us (3%)
    all_to_all x2, blocking collectives, on_device(): lax.all_to_all(summed.reshape(n, summed.shape[0] // n, d), axis, split_ax...  74.4 us
    all_to_all x1, waiting for transfers between devices, on_device(): lax.all_to_all(jnp.concatenate([y_rows, dh_rows], axis=1).reshape(groups,...  25.8 us
    all_to_all x1, waiting for transfers between devices, on_device(): lax.all_to_all(send, 'expert', split_axis=0, concat_axis=0, tiled=True)  15.8 us
    all_gather x1, waiting for transfers between devices, on_device(): weight = lax.all_gather(down_weight, DP, axis=1, tiled=True)[0]  11.9 us
    all_to_all x1, starting transfers between devices, on_device(): lax.all_to_all(summed.reshape(n, summed.shape[0] // n, d), axis, split_ax...  7.63 us
    all_to_all x1, starting transfers between devices, on_device(): lax.all_to_all(send, 'expert', split_axis=0, concat_axis=0, tiled=True)  7.31 us
    all_to_all x1, starting transfers between devices, on_device(): lax.all_to_all(jnp.concatenate([y_rows, dh_rows], axis=1).reshape(groups,...  4.89 us
  transfers between devices with their start and end apart: 4, of which 3 were waited for; matrix products, arithmetic and copies ran while one was open for 4% of the time, Pallas kernels for 0%

profile of v3, /device:TPU:1, one launch (start us, length us, event | category | flops | bytes accessed | tf_op | source)
XLA Modules:
  0.0 179.0 jit_solution(14146072485218985851)
XLA Ops:
  7.2 0.7 fusion.16
  7.9 0.2 reduce_window_sum.11
  8.1 0.8 select_reduce_fusion
  8.9 0.7 multiply_add_fusion
  10.2 0.0 copy-start.2
  10.3 2.3 %convolution_convert_fusion = bf16[256,1792]{1,0:T(8,128)(2,1)} fusion(bf16[128,1024]{1,0:T(8,128)(2,1)} %param.6, bf16[128,768]{1,0:T(8,128)(2,1)} %param.5, s32[128]{0:T(128)S(1)} %multiply_add_fusion, pred[128]{0:T(512)(128)(4,1)S(1)} %iota_compare_fusion.2), kind=kOutput, calls=%fused_computation | convolution fusion | flops 118882304 | bytes 1376896 | tf_op jit(solution)/shard_map/dot_general | solution.py:27
  12.6 7.3 %all-to-all-start = ((bf16[8,32,1792]{2,1,0:T(8,128)(2,1)}), bf16[8,32,1792]{2,1,0:T(8,128)(2,1)S(1)}, u32[]{:S(2)}, u32[]{:S(2)}) async-start(bf16[8,32,1792]{2,1,0:T(8,128)(2,1)} %bitcast.2), calls=%async_computation | async-start | bytes 1835008 | tf_op jit(solution)/shard_map/all_to_all | solution.py:32
  19.9 0.0 all-gather.2.cloned.1.call-start
  19.9 0.6 copy.18
  20.6 0.0 all-gather.2.cloned.1.call-update
  20.6 15.8 %all-to-all-done = bf16[8,32,1792]{2,1,0:T(8,128)(2,1)S(1)} async-done(((bf16[8,32,1792]{2,1,0:T(8,128)(2,1)}), bf16[8,32,1792]{2,1,0:T(8,128)(2,1)S(1)}, u32[]{:S(2)}, u32[]{:S(2)}) %all-to-all-start) | async-done | bytes 917536 | tf_op jit(solution)/shard_map/all_to_all | solution.py:32
  36.4 0.2 copy.16
  36.6 0.1 reshape.46
  36.8 0.1 reshape.47
  36.9 0.4 copy-done
  37.3 0.6 fusion.1
  37.9 17.2 %all_to_all.25 = f32[2,384,1024]{2,1,0:T(8,128)S(1)} all-to-all(f32[2,384,1024]{2,1,0:T(8,128)S(1)} %fusion.1), channel_id=1, replica_groups=mesh['expert'=8,'y'=8,'z'=8,'c'=2] {'c'}, dimensions={0} | all-to-all | bytes 6291456 | tf_op jit(solution)/shard_map/all_to_all | solution.py:42
  55.1 1.5 reduce_sum.37
  56.6 57.2 %all_to_all.26 = f32[8,48,1024]{2,1,0:T(8,128)S(1)} all-to-all(f32[8,48,1024]{2,1,0:T(8,128)} %bitcast.26), channel_id=1, replica_groups=mesh['expert'=8,'y'=8,'z'=8,'c'=2] {'z'}, dimensions={0} | all-to-all | bytes 3145728 | tf_op jit(solution)/shard_map/all_to_all | solution.py:42
  113.8 0.1 reduce_sum.38
  113.9 0.7 reshape.49
  114.6 7.6 %all-to-all-start.3 = ((f32[8,6,1024]{2,1,0:T(8,128)}), f32[8,6,1024]{2,1,0:T(8,128)S(1)}, u32[]{:S(2)}, u32[]{:S(2)}) async-start(f32[8,6,1024]{2,1,0:T(8,128)} %reshape.49), calls=%async_computation.3 | async-start | bytes 524288 | tf_op jit(solution)/shard_map/all_to_all | solution.py:42
  122.3 11.9 %all-gather.2.cloned.1.call-done = bf16[1,768,1024]{2,0,1:T(2,128)(2,1)} async-done(((bf16[1,6,1024]{2,0,1:T(2,128)(2,1)}), bf16[1,768,1024]{2,0,1:T(2,128)(2,1)}) %all-gather.2.cloned.1.call-update) | async-done | bytes 1572880 | tf_op jit(solution)/shard_map/all_gather | solution.py:31
  134.2 2.5 %copy.21 = bf16[1,768,1024]{2,1,0:T(8,128)(2,1)S(1)} copy(bf16[1,768,1024]{2,0,1:T(2,128)(2,1)} %all-gather.2.cloned.1.call-done) | data formatting | bytes 3145728
  136.7 0.6 convolution_convert_fusion.1
  137.3 0.6 convolution_convert_fusion.2
  137.9 1.0 pad_maximum_fusion
  138.9 4.9 %all-to-all-start.4 = ((bf16[8,32,1792]{2,1,0:T(8,128)(2,1)}), bf16[8,32,1792]{2,1,0:T(8,128)(2,1)S(1)}, u32[]{:S(2)}, u32[]{:S(2)}) async-start(bf16[8,32,1792]{2,1,0:T(8,128)(2,1)} %bitcast.9), calls=%async_computation.4 | async-start | bytes 1835008 | tf_op jit(solution)/shard_map/all_to_all | solution.py:51
  143.8 0.6 broadcast_in_dim.2
  144.4 25.8 %all-to-all-done.4 = bf16[8,32,1792]{2,1,0:T(8,128)(2,1)S(1)} async-done(((bf16[8,32,1792]{2,1,0:T(8,128)(2,1)}), bf16[8,32,1792]{2,1,0:T(8,128)(2,1)S(1)}, u32[]{:S(2)}, u32[]{:S(2)}) %all-to-all-start.4) | async-done | bytes 917536 | tf_op jit(solution)/shard_map/all_to_all | solution.py:51
  170.2 0.9 convolution_convert_fusion.4
  171.1 1.0 convolution_convert_fusion.3
  (9 shorter events, 0.1 us)
Async XLA Ops:
  10.2 9.7 %copy-start.2 = (bf16[1,6,1024]{2,1,0:T(8,128)(2,1)S(1)}, bf16[1,6,1024]{2,1,0:T(8,128)(2,1)}, u32[]{:S(2)}) copy-start(bf16[1,6,1024]{2,1,0:T(8,128)(2,1)} %param.9) | copy-start | bytes 36868
  12.6 23.8 %all-to-all-start = ((bf16[8,32,1792]{2,1,0:T(8,128)(2,1)}), bf16[8,32,1792]{2,1,0:T(8,128)(2,1)S(1)}, u32[]{:S(2)}, u32[]{:S(2)}) async-start(bf16[8,32,1792]{2,1,0:T(8,128)(2,1)} %bitcast.2), calls=%async_computation | async-start | bytes 1835008 | tf_op jit(solution)/shard_map/all_to_all | solution.py:32
  19.9 114.3 %all-gather.2.cloned.1.call-start = ((), (), s32[]{:S(2)}) async-start(), calls=%async_computation.5 | async-start | bytes 3170304 | tf_op jit(solution)/shard_map/all_gather | solution.py:31
  36.4 0.9 copy-start
  114.6 22.0 %all-to-all-start.3 = ((f32[8,6,1024]{2,1,0:T(8,128)}), f32[8,6,1024]{2,1,0:T(8,128)S(1)}, u32[]{:S(2)}, u32[]{:S(2)}) async-start(f32[8,6,1024]{2,1,0:T(8,128)} %reshape.49), calls=%async_computation.3 | async-start | bytes 524288 | tf_op jit(solution)/shard_map/all_to_all | solution.py:42
  122.3 14.4 %copy-start.1 = (bf16[8,32,1792]{2,1,0:T(8,128)(2,1)S(1)}, bf16[8,32,1792]{2,1,0:T(8,128)(2,1)}, u32[]{:S(2)}) copy-start(bf16[8,32,1792]{2,1,0:T(8,128)(2,1)} %copy-done) | copy-start | bytes 2752516
  138.9 31.3 %all-to-all-start.4 = ((bf16[8,32,1792]{2,1,0:T(8,128)(2,1)}), bf16[8,32,1792]{2,1,0:T(8,128)(2,1)S(1)}, u32[]{:S(2)}, u32[]{:S(2)}) async-start(bf16[8,32,1792]{2,1,0:T(8,128)(2,1)} %bitcast.9), calls=%async_computation.4 | async-start | bytes 1835008 | tf_op jit(solution)/shard_map/all_to_all | solution.py:51
Sparse Core Ops, SparseCore 0:
  25.6 108.5 all-gather.1

commit v4 on v3

--- a/solution.py
+++ b/solution.py
@@ -28,7 +28,14 @@
         .astype(jnp.bfloat16)
         .reshape(groups, CAP, ff + d)
     )
-    weight = lax.all_gather(down_weight, DP, axis=1, tiled=True)[0]
+    weight = down_weight[0]
+    steps = (("y", 4), ("z", 4), ("y", 2), ("z", 2), ("y", 1), ("z", 1), ("c", 1))
+    for axis, bit in steps:
+        n = lax.axis_size(axis)
+        recv = lax.ppermute(weight, axis, [(i, i ^ bit) for i in range(n)])
+        low = (lax.axis_index(axis) // bit) % 2 == 0
+        weight = jnp.concatenate([jnp.where(low, weight, recv), jnp.where(low, recv, weight)], axis=0)
+    weight = weight.reshape(2, 2, 2, 2, 2, 2, 2, -1, d).transpose(6, 4, 2, 5, 3, 1, 0, 7, 8).reshape(ff, d)
     recv = lax.all_to_all(send, "expert", split_axis=0, concat_axis=0, tiled=True).reshape(width, ff + d)
     h_rows = recv[:, :ff]
     g_rows = recv[:, ff:]

time: 179 us -> 182 us (1.017)
  blocking collectives: 74.4 us -> 8.93 us
  starting transfers between devices: 19.9 us -> 71.2 us
  waiting for transfers between devices: 53.5 us -> 75.1 us
  between operations: 14.8 us -> 1.74 us
  local copies, waits for them, and re-layouts: 5.38 us -> 9 us
  other arithmetic: 5.05 us -> 8.42 us
    all_to_all x2 -> x1, blocking collectives: 74.4 us -> 8.93 us  [on_device(): lax.all_to_all(summed.reshape(n, summed.shape[0] // n, d), axis, split_ax...]
    ppermute x0 -> x7, waiting for transfers between devices: none -> 48.9 us  [on_device(): recv = lax.ppermute(weight, axis, [(i, i ^ bit) for i in range(n)])]
    ppermute x0 -> x7, starting transfers between devices: none -> 41.6 us  [on_device(): recv = lax.ppermute(weight, axis, [(i, i ^ bit) for i in range(n)])]
    all_to_all x1, waiting for transfers between devices: 15.8 us -> 0.01 us  [on_device(): lax.all_to_all(send, 'expert', split_axis=0, concat_axis=0, tiled=True)]
    all_gather x1 -> x0, waiting for transfers between devices: 11.9 us -> none  [on_device(): weight = lax.all_gather(down_weight, DP, axis=1, tiled=True)[0]]
    all_to_all x1 -> x2, starting transfers between devices: 7.63 us -> 18.7 us  [on_device(): lax.all_to_all(summed.reshape(n, summed.shape[0] // n, d), axis, split_ax...]
    reshape x0 -> x2, local copies, waits for them, and re-layouts: none -> 5.16 us  [on_device(): weight.reshape(2, 2, 2, 2, 2, 2, 2, -1, d)]
    unnamed x8 -> x6, local copies, waits for them, and re-layouts: 3.52 us -> 0.39 us
  transfers between devices with their start and end apart: 4 -> 11, of which waited for: 3 -> 7; matrix products, arithmetic and copies ran while one was open for 4% -> 8% of each run, Pallas kernels for 0% -> 0%
where the time goes in v4:
time: 182 us; the launch traced here: 180 us
  waiting for transfers between devices  75.1 us (41%)
  starting transfers between devices  71.2 us (39%)
  local copies, waits for them, and re-layouts  9 us (5%)
  blocking collectives  8.93 us (5%)
  other arithmetic  8.42 us (5%)
  matrix products  6 us (3%)
    ppermute x7, waiting for transfers between devices, on_device(): recv = lax.ppermute(weight, axis, [(i, i ^ bit) for i in range(n)])  48.9 us
    ppermute x7, starting transfers between devices, on_device(): recv = lax.ppermute(weight, axis, [(i, i ^ bit) for i in range(n)])  41.6 us
    all_to_all x1, waiting for transfers between devices, on_device(): lax.all_to_all(jnp.concatenate([y_rows, dh_rows], axis=1).reshape(groups,...  23.4 us
    all_to_all x2, starting transfers between devices, on_device(): lax.all_to_all(summed.reshape(n, summed.shape[0] // n, d), axis, split_ax...  18.7 us
    all_to_all x1, blocking collectives, on_device(): lax.all_to_all(summed.reshape(n, summed.shape[0] // n, d), axis, split_ax...  8.93 us
    all_to_all x1, starting transfers between devices, on_device(): lax.all_to_all(send, 'expert', split_axis=0, concat_axis=0, tiled=True)  7.31 us
    reshape x2, local copies, waits for them, and re-layouts, on_device(): weight.reshape(2, 2, 2, 2, 2, 2, 2, -1, d)  5.16 us
  transfers between devices with their start and end apart: 11, of which 7 were waited for; matrix products, arithmetic and copies ran while one was open for 8% of the time, Pallas kernels for 0%

profile of v4, /device:TPU:1, one launch (start us, length us, event | category | flops | bytes accessed | tf_op | source)
XLA Modules:
  0.0 180.4 jit_solution(4596450345207095854)
XLA Ops:
  0.6 0.7 fusion.16
  1.5 0.8 select_reduce_fusion
  3.7 2.3 %convolution_convert_fusion = bf16[256,1792]{1,0:T(8,128)(2,1)} fusion(bf16[128,1024]{1,0:T(8,128)(2,1)} %param.6, bf16[128,768]{1,0:T(8,128)(2,1)} %param.5, s32[128]{0:T(128)S(1)} %multiply_add_fusion, pred[128]{0:T(512)(128)(4,1)S(1)} %iota_compare_fusion.2), kind=kOutput, calls=%fused_computation | convolution fusion | flops 118882304 | bytes 1376896 | tf_op jit(solution)/shard_map/dot_general | solution.py:27
  6.1 7.3 %all-to-all-start = ((bf16[8,32,1792]{2,1,0:T(8,128)(2,1)}), bf16[8,32,1792]{2,1,0:T(8,128)(2,1)S(1)}, u32[]{:S(2)}, u32[]{:S(2)}) async-start(bf16[8,32,1792]{2,1,0:T(8,128)(2,1)} %bitcast.2), calls=%async_computation | async-start | bytes 1835008 | tf_op jit(solution)/shard_map/all_to_all | solution.py:39
  13.4 7.9 %collective-permute-start = (bf16[6,1024]{1,0:T(8,128)(2,1)S(1)}, bf16[6,1024]{1,0:T(8,128)(2,1)S(1)}, u32[]{:S(2)}, u32[]{:S(2)}) collective-permute-start(bf16[6,1024]{1,0:T(8,128)(2,1)S(1)} %bitcast.37), channel_id=1, source_target_pairs={{0,64},{16,80},{32,96},{48,112},{64,0},{80,16},{96,32},{112,48},{1... | collective-permute-start | bytes 36872 | tf_op jit(solution)/shard_map/ppermute | solution.py:35
  21.3 1.1 collective-permute-done
  22.4 14.3 %collective-permute-start.1 = (bf16[12,1024]{1,0:T(8,128)(2,1)S(1)}, bf16[12,1024]{1,0:T(8,128)(2,1)S(1)}, u32[]{:S(2)}, u32[]{:S(2)}) collective-permute-start(bf16[12,1024]{1,0:T(8,128)(2,1)S(1)} %pad_maximum_fusion.7), channel_id=1, source_target_pairs={{0,8},{2,10},{4,12},{6,14},{8,0},{10,2},{12,4},{14,6},{1,9},{3,11}... | collective-permute-start | bytes 73736 | tf_op jit(solution)/shard_map/ppermute | solution.py:35
  36.8 1.2 collective-permute-done.1
  38.1 4.1 %collective-permute-start.2 = (bf16[24,1024]{1,0:T(8,128)(2,1)S(1)}, bf16[24,1024]{1,0:T(8,128)(2,1)S(1)}, u32[]{:S(2)}, u32[]{:S(2)}) collective-permute-start(bf16[24,1024]{1,0:T(8,128)(2,1)S(1)} %pad_maximum_fusion.6), channel_id=1, source_target_pairs={{0,32},{16,48},{32,0},{48,16},{64,96},{80,112},{96,64},{112,80},{1... | collective-permute-start | bytes 147464 | tf_op jit(solution)/shard_map/ppermute | solution.py:35
  43.7 8.9 %all_to_all.25 = f32[2,384,1024]{2,1,0:T(8,128)S(1)} all-to-all(f32[2,384,1024]{2,1,0:T(8,128)S(1)} %fusion.1), channel_id=1, replica_groups=mesh['expert'=8,'y'=8,'z'=8,'c'=2] {'c'}, dimensions={0} | all-to-all | bytes 6291456 | tf_op jit(solution)/shard_map/all_to_all | solution.py:49
  52.6 1.6 reduce_sum.37
  54.2 11.4 %all-to-all-start.2 = ((f32[8,48,1024]{2,1,0:T(8,128)}), f32[8,48,1024]{2,1,0:T(8,128)S(1)}, u32[]{:S(2)}, u32[]{:S(2)}) async-start(f32[8,48,1024]{2,1,0:T(8,128)} %bitcast.28), calls=%async_computation.2 | async-start | bytes 3145728 | tf_op jit(solution)/shard_map/all_to_all | solution.py:49
  65.7 4.3 %collective-permute-start.3 = (bf16[48,1024]{1,0:T(8,128)(2,1)S(1)}, bf16[48,1024]{1,0:T(8,128)(2,1)S(1)}, u32[]{:S(2)}, u32[]{:S(2)}) collective-permute-start(bf16[48,1024]{1,0:T(8,128)(2,1)S(1)} %pad_maximum_fusion.5), channel_id=1, source_target_pairs={{0,4},{2,6},{4,0},{6,2},{8,12},{10,14},{12,8},{14,10},{1,5},{3,7},... | collective-permute-start | bytes 294920 | tf_op jit(solution)/shard_map/ppermute | solution.py:35
  70.0 35.9 %collective-permute-done.3 = bf16[48,1024]{1,0:T(8,128)(2,1)S(1)} collective-permute-done((bf16[48,1024]{1,0:T(8,128)(2,1)S(1)}, bf16[48,1024]{1,0:T(8,128)(2,1)S(1)}, u32[]{:S(2)}, u32[]{:S(2)}) %collective-permute-start.3) | collective-permute-done | bytes 98336 | tf_op jit(solution)/shard_map/ppermute | solution.py:35
  106.0 3.3 %collective-permute-start.4 = (bf16[96,1024]{1,0:T(8,128)(2,1)S(1)}, bf16[96,1024]{1,0:T(8,128)(2,1)S(1)}, u32[]{:S(2)}, u32[]{:S(2)}) collective-permute-start(bf16[96,1024]{1,0:T(8,128)(2,1)S(1)} %pad_maximum_fusion.4), channel_id=1, source_target_pairs={{0,16},{16,0},{32,48},{48,32},{64,80},{80,64},{96,112},{112,96},{1... | collective-permute-start | bytes 589832 | tf_op jit(solution)/shard_map/ppermute | solution.py:35
  109.3 3.1 %collective-permute-done.4 = bf16[96,1024]{1,0:T(8,128)(2,1)S(1)} collective-permute-done((bf16[96,1024]{1,0:T(8,128)(2,1)S(1)}, bf16[96,1024]{1,0:T(8,128)(2,1)S(1)}, u32[]{:S(2)}, u32[]{:S(2)}) %collective-permute-start.4) | collective-permute-done | bytes 196640 | tf_op jit(solution)/shard_map/ppermute | solution.py:35
  112.5 1.9 %collective-permute-start.5 = (bf16[192,1024]{1,0:T(8,128)(2,1)S(1)}, bf16[192,1024]{1,0:T(8,128)(2,1)S(1)}, u32[]{:S(2)}, u32[]{:S(2)}) collective-permute-start(bf16[192,1024]{1,0:T(8,128)(2,1)S(1)} %pad_maximum_fusion.3), channel_id=1, source_target_pairs={{0,2},{2,0},{4,6},{6,4},{8,10},{10,8},{12,14},{14,12},{1,3},{3,1},... | collective-permute-start | bytes 1179656 | tf_op jit(solution)/shard_map/ppermute | solution.py:35
  114.5 7.6 %collective-permute-done.5 = bf16[192,1024]{1,0:T(8,128)(2,1)S(1)} collective-permute-done((bf16[192,1024]{1,0:T(8,128)(2,1)S(1)}, bf16[192,1024]{1,0:T(8,128)(2,1)S(1)}, u32[]{:S(2)}, u32[]{:S(2)}) %collective-permute-start.5) | collective-permute-done | bytes 393248 | tf_op jit(solution)/shard_map/ppermute | solution.py:35
  122.3 5.8 %collective-permute-start.6 = (bf16[384,1024]{1,0:T(8,128)(2,1)S(1)}, bf16[384,1024]{1,0:T(8,128)(2,1)}, u32[]{:S(2)}, u32[]{:S(2)}) collective-permute-start(bf16[384,1024]{1,0:T(8,128)(2,1)S(1)} %pad_maximum_fusion.2), channel_id=1, source_target_pairs={{0,1},{1,0},{2,3},{3,2},{4,5},{5,4},{6,7},{7,6},{8,9},{9,8},{10,11... | collective-permute-start | bytes 2359304 | tf_op jit(solution)/shard_map/ppermute | solution.py:35
  128.2 0.7 reshape.55
  129.0 7.3 %all-to-all-start.3 = ((f32[8,6,1024]{2,1,0:T(8,128)}), f32[8,6,1024]{2,1,0:T(8,128)S(1)}, u32[]{:S(2)}, u32[]{:S(2)}) async-start(f32[8,6,1024]{2,1,0:T(8,128)} %reshape.55), calls=%async_computation.3 | async-start | bytes 524288 | tf_op jit(solution)/shard_map/all_to_all | solution.py:49
  136.3 1.5 broadcast_select_fusion.1
  137.8 1.3 pad_maximum_fusion
  139.1 2.5 %reshape.56 = bf16[2,2,2,2,2,2,2,6,1024]{8,7,6,5,4,3,2,1,0:T(8,128)(2,1)S(1)} reshape(bf16[768,1024]{1,0:T(8,128)(2,1)} %pad_maximum_fusion) | data formatting | bytes 3145728 | tf_op jit(solution)/shard_map/reshape | solution.py:38
  141.6 1.6 copy.13
  143.2 2.7 %reshape.57 = bf16[768,1024]{1,0:T(8,128)(2,1)S(1)} reshape(bf16[2,2,2,2,2,2,2,6,1024]{8,7,6,5,4,3,2,1,0:T(8,128)(2,1)} %copy.13) | data formatting | bytes 3145728 | tf_op jit(solution)/shard_map/reshape | solution.py:38
  145.8 2.8 %all-to-all-done.3 = f32[8,6,1024]{2,1,0:T(8,128)S(1)} async-done(((f32[8,6,1024]{2,1,0:T(8,128)}), f32[8,6,1024]{2,1,0:T(8,128)S(1)}, u32[]{:S(2)}, u32[]{:S(2)}) %all-to-all-start.3) | async-done | bytes 196640 | tf_op jit(solution)/shard_map/all_to_all | solution.py:49
  149.9 1.0 pad_maximum_fusion.1
  150.9 3.6 %all-to-all-start.4 = ((bf16[8,32,1792]{2,1,0:T(8,128)(2,1)}), bf16[8,32,1792]{2,1,0:T(8,128)(2,1)S(1)}, u32[]{:S(2)}, u32[]{:S(2)}) async-start(bf16[8,32,1792]{2,1,0:T(8,128)(2,1)} %bitcast.11), calls=%async_computation.4 | async-start | bytes 1835008 | tf_op jit(solution)/shard_map/all_to_all | solution.py:58
  155.0 23.4 %all-to-all-done.4 = bf16[8,32,1792]{2,1,0:T(8,128)(2,1)S(1)} async-done(((bf16[8,32,1792]{2,1,0:T(8,128)(2,1)}), bf16[8,32,1792]{2,1,0:T(8,128)(2,1)S(1)}, u32[]{:S(2)}, u32[]{:S(2)}) %all-to-all-start.4) | async-done | bytes 917536 | tf_op jit(solution)/shard_map/all_to_all | solution.py:58
  178.5 1.0 convolution_convert_fusion.3
  179.5 0.9 convolution_convert_fusion.4
  (36 shorter events, 4.8 us)
Async XLA Ops:
  3.7 9.7 %copy-start.2 = (bf16[1,6,1024]{2,1,0:T(8,128)(2,1)S(1)}, bf16[1,6,1024]{2,1,0:T(8,128)(2,1)}, u32[]{:S(2)}) copy-start(bf16[1,6,1024]{2,1,0:T(8,128)(2,1)} %param.9) | copy-start | bytes 36868
  6.1 36.1 %all-to-all-start = ((bf16[8,32,1792]{2,1,0:T(8,128)(2,1)}), bf16[8,32,1792]{2,1,0:T(8,128)(2,1)S(1)}, u32[]{:S(2)}, u32[]{:S(2)}) async-start(bf16[8,32,1792]{2,1,0:T(8,128)(2,1)} %bitcast.2), calls=%async_computation | async-start | bytes 1835008 | tf_op jit(solution)/shard_map/all_to_all | solution.py:39
  13.4 9.0 %collective-permute-start = (bf16[6,1024]{1,0:T(8,128)(2,1)S(1)}, bf16[6,1024]{1,0:T(8,128)(2,1)S(1)}, u32[]{:S(2)}, u32[]{:S(2)}) collective-permute-start(bf16[6,1024]{1,0:T(8,128)(2,1)S(1)} %bitcast.37), channel_id=1, source_target_pairs={{0,64},{16,80},{32,96},{48,112},{64,0},{80,16},{96,32},{112,48},{1... | collective-permute-start | bytes 36872 | tf_op jit(solution)/shard_map/ppermute | solution.py:35
  22.4 15.6 %collective-permute-start.1 = (bf16[12,1024]{1,0:T(8,128)(2,1)S(1)}, bf16[12,1024]{1,0:T(8,128)(2,1)S(1)}, u32[]{:S(2)}, u32[]{:S(2)}) collective-permute-start(bf16[12,1024]{1,0:T(8,128)(2,1)S(1)} %pad_maximum_fusion.7), channel_id=1, source_target_pairs={{0,8},{2,10},{4,12},{6,14},{8,0},{10,2},{12,4},{14,6},{1,9},{3,11}... | collective-permute-start | bytes 73736 | tf_op jit(solution)/shard_map/ppermute | solution.py:35
  38.1 27.6 %collective-permute-start.2 = (bf16[24,1024]{1,0:T(8,128)(2,1)S(1)}, bf16[24,1024]{1,0:T(8,128)(2,1)S(1)}, u32[]{:S(2)}, u32[]{:S(2)}) collective-permute-start(bf16[24,1024]{1,0:T(8,128)(2,1)S(1)} %pad_maximum_fusion.6), channel_id=1, source_target_pairs={{0,32},{16,48},{32,0},{48,16},{64,96},{80,112},{96,64},{112,80},{1... | collective-permute-start | bytes 147464 | tf_op jit(solution)/shard_map/ppermute | solution.py:35
  42.2 0.9 copy-start
  54.2 73.9 %all-to-all-start.2 = ((f32[8,48,1024]{2,1,0:T(8,128)}), f32[8,48,1024]{2,1,0:T(8,128)S(1)}, u32[]{:S(2)}, u32[]{:S(2)}) async-start(f32[8,48,1024]{2,1,0:T(8,128)} %bitcast.28), calls=%async_computation.2 | async-start | bytes 3145728 | tf_op jit(solution)/shard_map/all_to_all | solution.py:49
  65.7 40.2 %collective-permute-start.3 = (bf16[48,1024]{1,0:T(8,128)(2,1)S(1)}, bf16[48,1024]{1,0:T(8,128)(2,1)S(1)}, u32[]{:S(2)}, u32[]{:S(2)}) collective-permute-start(bf16[48,1024]{1,0:T(8,128)(2,1)S(1)} %pad_maximum_fusion.5), channel_id=1, source_target_pairs={{0,4},{2,6},{4,0},{6,2},{8,12},{10,14},{12,8},{14,10},{1,5},{3,7},... | collective-permute-start | bytes 294920 | tf_op jit(solution)/shard_map/ppermute | solution.py:35
  106.0 6.4 %collective-permute-start.4 = (bf16[96,1024]{1,0:T(8,128)(2,1)S(1)}, bf16[96,1024]{1,0:T(8,128)(2,1)S(1)}, u32[]{:S(2)}, u32[]{:S(2)}) collective-permute-start(bf16[96,1024]{1,0:T(8,128)(2,1)S(1)} %pad_maximum_fusion.4), channel_id=1, source_target_pairs={{0,16},{16,0},{32,48},{48,32},{64,80},{80,64},{96,112},{112,96},{1... | collective-permute-start | bytes 589832 | tf_op jit(solution)/shard_map/ppermute | solution.py:35
  112.5 9.5 %collective-permute-start.5 = (bf16[192,1024]{1,0:T(8,128)(2,1)S(1)}, bf16[192,1024]{1,0:T(8,128)(2,1)S(1)}, u32[]{:S(2)}, u32[]{:S(2)}) collective-permute-start(bf16[192,1024]{1,0:T(8,128)(2,1)S(1)} %pad_maximum_fusion.3), channel_id=1, source_target_pairs={{0,2},{2,0},{4,6},{6,4},{8,10},{10,8},{12,14},{14,12},{1,3},{3,1},... | collective-permute-start | bytes 1179656 | tf_op jit(solution)/shard_map/ppermute | solution.py:35
  122.3 14.0 %collective-permute-start.6 = (bf16[384,1024]{1,0:T(8,128)(2,1)S(1)}, bf16[384,1024]{1,0:T(8,128)(2,1)}, u32[]{:S(2)}, u32[]{:S(2)}) collective-permute-start(bf16[384,1024]{1,0:T(8,128)(2,1)S(1)} %pad_maximum_fusion.2), channel_id=1, source_target_pairs={{0,1},{1,0},{2,3},{3,2},{4,5},{5,4},{6,7},{7,6},{8,9},{9,8},{10,11... | collective-permute-start | bytes 2359304 | tf_op jit(solution)/shard_map/ppermute | solution.py:35
  129.0 19.6 %all-to-all-start.3 = ((f32[8,6,1024]{2,1,0:T(8,128)}), f32[8,6,1024]{2,1,0:T(8,128)S(1)}, u32[]{:S(2)}, u32[]{:S(2)}) async-start(f32[8,6,1024]{2,1,0:T(8,128)} %reshape.55), calls=%async_computation.3 | async-start | bytes 524288 | tf_op jit(solution)/shard_map/all_to_all | solution.py:49
  143.2 5.5 %copy-start.1 = (bf16[8,32,1792]{2,1,0:T(8,128)(2,1)S(1)}, bf16[8,32,1792]{2,1,0:T(8,128)(2,1)}, u32[]{:S(2)}) copy-start(bf16[8,32,1792]{2,1,0:T(8,128)(2,1)} %copy-done) | copy-start | bytes 2752516
  150.9 27.6 %all-to-all-start.4 = ((bf16[8,32,1792]{2,1,0:T(8,128)(2,1)}), bf16[8,32,1792]{2,1,0:T(8,128)(2,1)S(1)}, u32[]{:S(2)}, u32[]{:S(2)}) async-start(bf16[8,32,1792]{2,1,0:T(8,128)(2,1)} %bitcast.11), calls=%async_computation.4 | async-start | bytes 1835008 | tf_op jit(solution)/shard_map/all_to_all | solution.py:58

commit v5 on v4

--- a/solution.py
+++ b/solution.py
@@ -35,26 +35,32 @@
         recv = lax.ppermute(weight, axis, [(i, i ^ bit) for i in range(n)])
         low = (lax.axis_index(axis) // bit) % 2 == 0
         weight = jnp.concatenate([jnp.where(low, weight, recv), jnp.where(low, recv, weight)], axis=0)
-    weight = weight.reshape(2, 2, 2, 2, 2, 2, 2, -1, d).transpose(6, 4, 2, 5, 3, 1, 0, 7, 8).reshape(ff, d)
     recv = lax.all_to_all(send, "expert", split_axis=0, concat_axis=0, tiled=True).reshape(width, ff + d)
     h_rows = recv[:, :ff]
     g_rows = recv[:, ff:]
-    rows_dev = ff // (ny * nz * nc)
-    h_perm = h_rows.reshape(width, ny, nz, nc, rows_dev).transpose(0, 3, 2, 1, 4).reshape(width, ff)
+    def order(x, axes):
+        return x.reshape((width,) + (2,) * 7 + (-1,)).transpose((0,) + axes + (8,)).reshape(width, ff)
+
     partial_grad = lax.dot_general(
-        h_perm, g_rows, (((0,), (0,)), ((), ())), preferred_element_type=jnp.float32
+        order(h_rows, (7, 3, 6, 2, 5, 1, 4)), g_rows, (((0,), (0,)), ((), ())),
+        preferred_element_type=jnp.float32,
     )
     summed = partial_grad
-    for axis, n in (("c", nc), ("z", nz), ("y", ny)):
-        parts = lax.all_to_all(
-            summed.reshape(n, summed.shape[0] // n, d), axis, split_axis=0, concat_axis=0, tiled=True
-        )
-        summed = jnp.sum(parts, axis=0)
+    for axis, bit in (("c", 1), ("y", 1), ("z", 1), ("y", 2), ("z", 2), ("y", 4), ("z", 4)):
+        n = lax.axis_size(axis)
+        half = summed.shape[0] // 2
+        upper = (lax.axis_index(axis) // bit) % 2
+        keep = lax.dynamic_slice_in_dim(summed, upper * half, half)
+        send = lax.dynamic_slice_in_dim(summed, (1 - upper) * half, half)
+        summed = keep + lax.ppermute(send, axis, [(i, i ^ bit) for i in range(n)])
     summed, weight = lax.optimization_barrier((summed, weight))
-    y_rows = jnp.dot(h_rows, weight, preferred_element_type=jnp.float32).astype(jnp.bfloat16)
+    y_rows = jnp.dot(
+        order(h_rows, (7, 6, 3, 5, 2, 4, 1)), weight, preferred_element_type=jnp.float32
+    ).astype(jnp.bfloat16)
     dh_rows = lax.dot_general(
         g_rows, weight, (((1,), (1,)), ((), ())), preferred_element_type=jnp.float32
     ).astype(jnp.bfloat16)
+    dh_rows = order(dh_rows, (7, 5, 3, 6, 4, 2, 1))
     back = lax.all_to_all(
         jnp.concatenate([y_rows, dh_rows], axis=1).reshape(groups, CAP, d + ff),
         "expert",

time: 182 us -> 188 us (1.033)
  the two profiles are of different devices: /device:TPU:1 before, /device:TPU:16 now
where the time goes in v5:
time: 188 us; the launch traced here: 187 us
  starting transfers between devices  80.7 us (43%)
  waiting for transfers between devices  78.4 us (42%)
  local copies, waits for them, and re-layouts  9.8 us (5%)
  matrix products  8.08 us (4%)
  other arithmetic  8.06 us (4%)
  between operations  2.05 us (1%)
    ppermute x7, starting transfers between devices, on_device(): recv = lax.ppermute(weight, axis, [(i, i ^ bit) for i in range(n)])  40 us
    ppermute x7, starting transfers between devices, on_device(): summed = keep + lax.ppermute(send, axis, [(i, i ^ bit) for i in range(n)])  30.5 us
    all_to_all x1, waiting for transfers between devices, on_device(): lax.all_to_all(send, 'expert', split_axis=0, concat_axis=0, tiled=True)  25.9 us
    all_to_all x1, waiting for transfers between devices, on_device(): lax.all_to_all(jnp.concatenate([y_rows, dh_rows], axis=1).reshape(groups,...  22.3 us
    ppermute x7, waiting for transfers between devices, on_device(): summed = keep + lax.ppermute(send, axis, [(i, i ^ bit) for i in range(n)])  21.7 us
    ppermute x7, waiting for transfers between devices, on_device(): recv = lax.ppermute(weight, axis, [(i, i ^ bit) for i in range(n)])  8.49 us
    all_to_all x1, starting transfers between devices, on_device(): lax.all_to_all(send, 'expert', split_axis=0, concat_axis=0, tiled=True)  6.76 us
    unnamed x19, local copies, waits for them, and re-layouts  4.77 us
  transfers between devices with their start and end apart: 16, of which 11 were waited for; matrix products, arithmetic and copies ran while one was open for 3% of the time, Pallas kernels for 0%

profile of v5, /device:TPU:16, one launch (start us, length us, event | category | flops | bytes accessed | tf_op | source)
XLA Modules:
  0.0 187.1 jit_solution(6430910559099008193)
XLA Ops:
  3.7 2.4 %convolution_convert_fusion = bf16[256,1792]{1,0:T(8,128)(2,1)} fusion(bf16[128,1024]{1,0:T(8,128)(2,1)} %param.6, bf16[128,768]{1,0:T(8,128)(2,1)} %param.5, s32[128]{0:T(128)S(1)} %multiply_add_fusion, pred[128]{0:T(512)(128)(4,1)S(1)} %iota_compare_fusion.2), kind=kOutput, calls=%fused_computation | convolution fusion | flops 118882304 | bytes 1376896 | tf_op jit(solution)/shard_map/dot_general | solution.py:27
  6.1 6.8 %all-to-all-start = ((bf16[8,32,1792]{2,1,0:T(8,128)(2,1)}), bf16[8,32,1792]{2,1,0:T(8,128)(2,1)S(1)}, u32[]{:S(2)}, u32[]{:S(2)}) async-start(bf16[8,32,1792]{2,1,0:T(8,128)(2,1)} %bitcast.2), calls=%async_computation | async-start | bytes 1835008 | tf_op jit(solution)/shard_map/all_to_all | solution.py:38
  12.8 25.9 %all-to-all-done = bf16[8,32,1792]{2,1,0:T(8,128)(2,1)S(1)} async-done(((bf16[8,32,1792]{2,1,0:T(8,128)(2,1)}), bf16[8,32,1792]{2,1,0:T(8,128)(2,1)S(1)}, u32[]{:S(2)}, u32[]{:S(2)}) %all-to-all-start) | async-done | bytes 917536 | tf_op jit(solution)/shard_map/all_to_all | solution.py:38
  40.9 1.6 fusion.2
  42.6 1.3 constant_dynamic-slice_fusion.6
  43.8 1.9 %collective-permute-start = (f32[384,1024]{1,0:T(8,128)}, f32[384,1024]{1,0:T(8,128)}, u32[]{:S(2)}, u32[]{:S(2)}) collective-permute-start(f32[384,1024]{1,0:T(8,128)} %constant_dynamic-slice_fusion.6), channel_id=1, source_target_pairs={{0,1},{1,0},{2,3},{3,2},{4,5},{5,4},{6,7},{7,6},{8,9},{9,8},{10,11... | collective-permute-start | bytes 4718600 | tf_op jit(solution)/shard_map/ppermute | solution.py:55
  45.8 7.3 %collective-permute-start.7 = (bf16[6,1024]{1,0:T(8,128)(2,1)S(1)}, bf16[6,1024]{1,0:T(8,128)(2,1)S(1)}, u32[]{:S(2)}, u32[]{:S(2)}) collective-permute-start(bf16[6,1024]{1,0:T(8,128)(2,1)S(1)} %bitcast.39), channel_id=1, source_target_pairs={{0,64},{16,80},{32,96},{48,112},{64,0},{80,16},{96,32},{112,48},{1... | collective-permute-start | bytes 36872 | tf_op jit(solution)/shard_map/ppermute | solution.py:35
  53.1 2.3 %collective-permute-done.7 = bf16[6,1024]{1,0:T(8,128)(2,1)S(1)} collective-permute-done((bf16[6,1024]{1,0:T(8,128)(2,1)S(1)}, bf16[6,1024]{1,0:T(8,128)(2,1)S(1)}, u32[]{:S(2)}, u32[]{:S(2)}) %collective-permute-start.7) | collective-permute-done | bytes 12320 | tf_op jit(solution)/shard_map/ppermute | solution.py:35
  55.5 14.6 %collective-permute-start.8 = (bf16[12,1024]{1,0:T(8,128)(2,1)S(1)}, bf16[12,1024]{1,0:T(8,128)(2,1)S(1)}, u32[]{:S(2)}, u32[]{:S(2)}) collective-permute-start(bf16[12,1024]{1,0:T(8,128)(2,1)S(1)} %pad_maximum_fusion.7), channel_id=1, source_target_pairs={{0,8},{2,10},{4,12},{6,14},{8,0},{10,2},{12,4},{14,6},{1,9},{3,11}... | collective-permute-start | bytes 73736 | tf_op jit(solution)/shard_map/ppermute | solution.py:35
  70.1 1.8 collective-permute-done.8
  71.9 4.6 %collective-permute-start.9 = (bf16[24,1024]{1,0:T(8,128)(2,1)S(1)}, bf16[24,1024]{1,0:T(8,128)(2,1)S(1)}, u32[]{:S(2)}, u32[]{:S(2)}) collective-permute-start(bf16[24,1024]{1,0:T(8,128)(2,1)S(1)} %pad_maximum_fusion.6), channel_id=1, source_target_pairs={{0,32},{16,48},{32,0},{48,16},{64,96},{80,112},{96,64},{112,80},{1... | collective-permute-start | bytes 147464 | tf_op jit(solution)/shard_map/ppermute | solution.py:35
  76.6 1.7 dynamic-slice_add_fusion
  79.5 2.4 %collective-permute-start.1 = (f32[192,1024]{1,0:T(8,128)S(1)}, f32[192,1024]{1,0:T(8,128)S(1)}, u32[]{:S(2)}, u32[]{:S(2)}) collective-permute-start(f32[192,1024]{1,0:T(8,128)S(1)} %constant_dynamic-slice_fusion.5), channel_id=1, source_target_pairs={{0,16},{16,0},{32,48},{48,32},{64,80},{80,64},{96,112},{112,96},{1... | collective-permute-start | bytes 2359304 | tf_op jit(solution)/shard_map/ppermute | solution.py:55
  82.0 6.1 %collective-permute-start.10 = (bf16[48,1024]{1,0:T(8,128)(2,1)S(1)}, bf16[48,1024]{1,0:T(8,128)(2,1)S(1)}, u32[]{:S(2)}, u32[]{:S(2)}) collective-permute-start(bf16[48,1024]{1,0:T(8,128)(2,1)S(1)} %pad_maximum_fusion.5), channel_id=1, source_target_pairs={{0,4},{2,6},{4,0},{6,2},{8,12},{10,14},{12,8},{14,10},{1,5},{3,7},... | collective-permute-start | bytes 294920 | tf_op jit(solution)/shard_map/ppermute | solution.py:35
  88.2 2.5 %collective-permute-done.10 = bf16[48,1024]{1,0:T(8,128)(2,1)S(1)} collective-permute-done((bf16[48,1024]{1,0:T(8,128)(2,1)S(1)}, bf16[48,1024]{1,0:T(8,128)(2,1)S(1)}, u32[]{:S(2)}, u32[]{:S(2)}) %collective-permute-start.10) | collective-permute-done | bytes 98336 | tf_op jit(solution)/shard_map/ppermute | solution.py:35
  90.7 3.5 %collective-permute-start.11 = (bf16[96,1024]{1,0:T(8,128)(2,1)S(1)}, bf16[96,1024]{1,0:T(8,128)(2,1)S(1)}, u32[]{:S(2)}, u32[]{:S(2)}) collective-permute-start(bf16[96,1024]{1,0:T(8,128)(2,1)S(1)} %pad_maximum_fusion.4), channel_id=1, source_target_pairs={{0,16},{16,0},{32,48},{48,32},{64,80},{80,64},{96,112},{112,96},{1... | collective-permute-start | bytes 589832 | tf_op jit(solution)/shard_map/ppermute | solution.py:35
  94.3 6.9 %collective-permute-done.1 = f32[192,1024]{1,0:T(8,128)S(1)} collective-permute-done((f32[192,1024]{1,0:T(8,128)S(1)}, f32[192,1024]{1,0:T(8,128)S(1)}, u32[]{:S(2)}, u32[]{:S(2)}) %collective-permute-start.1) | collective-permute-done | bytes 786464 | tf_op jit(solution)/shard_map/ppermute | solution.py:55
  102.4 4.3 %collective-permute-start.2 = (f32[96,1024]{1,0:T(8,128)S(1)}, f32[96,1024]{1,0:T(8,128)S(1)}, u32[]{:S(2)}, u32[]{:S(2)}) collective-permute-start(f32[96,1024]{1,0:T(8,128)S(1)} %constant_dynamic-slice_fusion.4), channel_id=1, source_target_pairs={{0,2},{2,0},{4,6},{6,4},{8,10},{10,8},{12,14},{14,12},{1,3},{3,1},... | collective-permute-start | bytes 1179656 | tf_op jit(solution)/shard_map/ppermute | solution.py:55
  106.8 1.9 %collective-permute-start.12 = (bf16[192,1024]{1,0:T(8,128)(2,1)S(1)}, bf16[192,1024]{1,0:T(8,128)(2,1)S(1)}, u32[]{:S(2)}, u32[]{:S(2)}) collective-permute-start(bf16[192,1024]{1,0:T(8,128)(2,1)S(1)} %pad_maximum_fusion.3), channel_id=1, source_target_pairs={{0,2},{2,0},{4,6},{6,4},{8,10},{10,8},{12,14},{14,12},{1,3},{3,1},... | collective-permute-start | bytes 1179656 | tf_op jit(solution)/shard_map/ppermute | solution.py:35
  108.8 6.6 %collective-permute-done.2 = f32[96,1024]{1,0:T(8,128)S(1)} collective-permute-done((f32[96,1024]{1,0:T(8,128)S(1)}, f32[96,1024]{1,0:T(8,128)S(1)}, u32[]{:S(2)}, u32[]{:S(2)}) %collective-permute-start.2) | collective-permute-done | bytes 393248 | tf_op jit(solution)/shard_map/ppermute | solution.py:55
  115.4 2.3 %collective-permute-start.3 = (f32[48,1024]{1,0:T(8,128)S(1)}, f32[48,1024]{1,0:T(8,128)S(1)}, u32[]{:S(2)}, u32[]{:S(2)}) collective-permute-start(f32[48,1024]{1,0:T(8,128)S(1)} %constant_dynamic-slice_fusion.3), channel_id=1, source_target_pairs={{0,32},{16,48},{32,0},{48,16},{64,96},{80,112},{96,64},{112,80},{1... | collective-permute-start | bytes 589832 | tf_op jit(solution)/shard_map/ppermute | solution.py:55
  117.7 1.8 collective-permute-done.12
  119.8 1.9 %collective-permute-start.13 = (bf16[384,1024]{1,0:T(8,128)(2,1)S(1)}, bf16[384,1024]{1,0:T(8,128)(2,1)S(1)}, u32[]{:S(2)}, u32[]{:S(2)}) collective-permute-start(bf16[384,1024]{1,0:T(8,128)(2,1)S(1)} %pad_maximum_fusion.2), channel_id=1, source_target_pairs={{0,1},{1,0},{2,3},{3,2},{4,5},{5,4},{6,7},{7,6},{8,9},{9,8},{10,11... | collective-permute-start | bytes 2359304 | tf_op jit(solution)/shard_map/ppermute | solution.py:35
  121.8 2.2 %collective-permute-done.3 = f32[48,1024]{1,0:T(8,128)S(1)} collective-permute-done((f32[48,1024]{1,0:T(8,128)S(1)}, f32[48,1024]{1,0:T(8,128)S(1)}, u32[]{:S(2)}, u32[]{:S(2)}) %collective-permute-start.3) | collective-permute-done | bytes 196640 | tf_op jit(solution)/shard_map/ppermute | solution.py:55
  124.1 5.8 %collective-permute-start.4 = (f32[24,1024]{1,0:T(8,128)S(1)}, f32[24,1024]{1,0:T(8,128)S(1)}, u32[]{:S(2)}, u32[]{:S(2)}) collective-permute-start(f32[24,1024]{1,0:T(8,128)S(1)} %constant_dynamic-slice_fusion.2), channel_id=1, source_target_pairs={{0,4},{2,6},{4,0},{6,2},{8,12},{10,14},{12,8},{14,10},{1,5},{3,7},... | collective-permute-start | bytes 294920 | tf_op jit(solution)/shard_map/ppermute | solution.py:55
  129.9 2.5 %collective-permute-done.4 = f32[24,1024]{1,0:T(8,128)S(1)} collective-permute-done((f32[24,1024]{1,0:T(8,128)S(1)}, f32[24,1024]{1,0:T(8,128)S(1)}, u32[]{:S(2)}, u32[]{:S(2)}) %collective-permute-start.4) | collective-permute-done | bytes 98336 | tf_op jit(solution)/shard_map/ppermute | solution.py:55
  132.4 6.2 %collective-permute-start.5 = (f32[12,1024]{1,0:T(8,128)S(1)}, f32[12,1024]{1,0:T(8,128)S(1)}, u32[]{:S(2)}, u32[]{:S(2)}) collective-permute-start(f32[12,1024]{1,0:T(8,128)S(1)} %constant_dynamic-slice_fusion.1), channel_id=1, source_target_pairs={{0,64},{16,80},{32,96},{48,112},{64,0},{80,16},{96,32},{112,48},{1... | collective-permute-start | bytes 147464 | tf_op jit(solution)/shard_map/ppermute | solution.py:55
  139.0 3.5 %collective-permute-done.5 = f32[12,1024]{1,0:T(8,128)S(1)} collective-permute-done((f32[12,1024]{1,0:T(8,128)S(1)}, f32[12,1024]{1,0:T(8,128)S(1)}, u32[]{:S(2)}, u32[]{:S(2)}) %collective-permute-start.5) | collective-permute-done | bytes 49184 | tf_op jit(solution)/shard_map/ppermute | solution.py:55
  142.6 7.6 %collective-permute-start.6 = (f32[6,1024]{1,0:T(8,128)S(1)}, f32[6,1024]{1,0:T(8,128)S(1)}, u32[]{:S(2)}, u32[]{:S(2)}) collective-permute-start(f32[6,1024]{1,0:T(8,128)S(1)} %constant_dynamic-slice_fusion), channel_id=1, source_target_pairs={{0,8},{2,10},{4,12},{6,14},{8,0},{10,2},{12,4},{14,6},{1,9},{3,11}... | collective-permute-start | bytes 73736 | tf_op jit(solution)/shard_map/ppermute | solution.py:55
  156.1 1.6 convolution_convert_fusion.1
  158.7 3.6 %all-to-all-start.1 = ((bf16[8,32,1792]{2,1,0:T(8,128)(2,1)}), bf16[8,32,1792]{2,1,0:T(8,128)(2,1)S(1)}, u32[]{:S(2)}, u32[]{:S(2)}) async-start(bf16[8,32,1792]{2,1,0:T(8,128)(2,1)} %pad_maximum_fusion.1), calls=%async_computation.1 | async-start | bytes 1835008 | tf_op jit(solution)/shard_map/all_to_all | solution.py:64
  162.9 22.3 %all-to-all-done.1 = bf16[8,32,1792]{2,1,0:T(8,128)(2,1)S(1)} async-done(((bf16[8,32,1792]{2,1,0:T(8,128)(2,1)}), bf16[8,32,1792]{2,1,0:T(8,128)(2,1)S(1)}, u32[]{:S(2)}, u32[]{:S(2)}) %all-to-all-start.1) | async-done | bytes 917536 | tf_op jit(solution)/shard_map/all_to_all | solution.py:64
  (71 shorter events, 17.5 us)
Async XLA Ops:
  6.1 32.7 %all-to-all-start = ((bf16[8,32,1792]{2,1,0:T(8,128)(2,1)}), bf16[8,32,1792]{2,1,0:T(8,128)(2,1)S(1)}, u32[]{:S(2)}, u32[]{:S(2)}) async-start(bf16[8,32,1792]{2,1,0:T(8,128)(2,1)} %bitcast.2), calls=%async_computation | async-start | bytes 1835008 | tf_op jit(solution)/shard_map/all_to_all | solution.py:38
  38.8 0.9 copy-start.3
  40.0 0.8 copy-start.1
  42.5 3.2 %copy-start.8 = (bf16[1,6,1024]{2,1,0:T(8,128)(2,1)S(1)}, bf16[1,6,1024]{2,1,0:T(8,128)(2,1)}, u32[]{:S(2)}) copy-start(bf16[1,6,1024]{2,1,0:T(8,128)(2,1)} %param.9) | copy-start | bytes 36868
  43.8 32.7 %collective-permute-start = (f32[384,1024]{1,0:T(8,128)}, f32[384,1024]{1,0:T(8,128)}, u32[]{:S(2)}, u32[]{:S(2)}) collective-permute-start(f32[384,1024]{1,0:T(8,128)} %constant_dynamic-slice_fusion.6), channel_id=1, source_target_pairs={{0,1},{1,0},{2,3},{3,2},{4,5},{5,4},{6,7},{7,6},{8,9},{9,8},{10,11... | collective-permute-start | bytes 4718600 | tf_op jit(solution)/shard_map/ppermute | solution.py:55
  45.8 9.6 %collective-permute-start.7 = (bf16[6,1024]{1,0:T(8,128)(2,1)S(1)}, bf16[6,1024]{1,0:T(8,128)(2,1)S(1)}, u32[]{:S(2)}, u32[]{:S(2)}) collective-permute-start(bf16[6,1024]{1,0:T(8,128)(2,1)S(1)} %bitcast.39), channel_id=1, source_target_pairs={{0,64},{16,80},{32,96},{48,112},{64,0},{80,16},{96,32},{112,48},{1... | collective-permute-start | bytes 36872 | tf_op jit(solution)/shard_map/ppermute | solution.py:35
  55.5 16.4 %collective-permute-start.8 = (bf16[12,1024]{1,0:T(8,128)(2,1)S(1)}, bf16[12,1024]{1,0:T(8,128)(2,1)S(1)}, u32[]{:S(2)}, u32[]{:S(2)}) collective-permute-start(bf16[12,1024]{1,0:T(8,128)(2,1)S(1)} %pad_maximum_fusion.7), channel_id=1, source_target_pairs={{0,8},{2,10},{4,12},{6,14},{8,0},{10,2},{12,4},{14,6},{1,9},{3,11}... | collective-permute-start | bytes 73736 | tf_op jit(solution)/shard_map/ppermute | solution.py:35
  71.9 10.0 %collective-permute-start.9 = (bf16[24,1024]{1,0:T(8,128)(2,1)S(1)}, bf16[24,1024]{1,0:T(8,128)(2,1)S(1)}, u32[]{:S(2)}, u32[]{:S(2)}) collective-permute-start(bf16[24,1024]{1,0:T(8,128)(2,1)S(1)} %pad_maximum_fusion.6), channel_id=1, source_target_pairs={{0,32},{16,48},{32,0},{48,16},{64,96},{80,112},{96,64},{112,80},{1... | collective-permute-start | bytes 147464 | tf_op jit(solution)/shard_map/ppermute | solution.py:35
  78.3 1.2 copy-start
  79.5 21.6 %collective-permute-start.1 = (f32[192,1024]{1,0:T(8,128)S(1)}, f32[192,1024]{1,0:T(8,128)S(1)}, u32[]{:S(2)}, u32[]{:S(2)}) collective-permute-start(f32[192,1024]{1,0:T(8,128)S(1)} %constant_dynamic-slice_fusion.5), channel_id=1, source_target_pairs={{0,16},{16,0},{32,48},{48,32},{64,80},{80,64},{96,112},{112,96},{1... | collective-permute-start | bytes 2359304 | tf_op jit(solution)/shard_map/ppermute | solution.py:55
  82.0 8.7 %collective-permute-start.10 = (bf16[48,1024]{1,0:T(8,128)(2,1)S(1)}, bf16[48,1024]{1,0:T(8,128)(2,1)S(1)}, u32[]{:S(2)}, u32[]{:S(2)}) collective-permute-start(bf16[48,1024]{1,0:T(8,128)(2,1)S(1)} %pad_maximum_fusion.5), channel_id=1, source_target_pairs={{0,4},{2,6},{4,0},{6,2},{8,12},{10,14},{12,8},{14,10},{1,5},{3,7},... | collective-permute-start | bytes 294920 | tf_op jit(solution)/shard_map/ppermute | solution.py:35
  90.7 16.0 %collective-permute-start.11 = (bf16[96,1024]{1,0:T(8,128)(2,1)S(1)}, bf16[96,1024]{1,0:T(8,128)(2,1)S(1)}, u32[]{:S(2)}, u32[]{:S(2)}) collective-permute-start(bf16[96,1024]{1,0:T(8,128)(2,1)S(1)} %pad_maximum_fusion.4), channel_id=1, source_target_pairs={{0,16},{16,0},{32,48},{48,32},{64,80},{80,64},{96,112},{112,96},{1... | collective-permute-start | bytes 589832 | tf_op jit(solution)/shard_map/ppermute | solution.py:35
  102.4 12.9 %collective-permute-start.2 = (f32[96,1024]{1,0:T(8,128)S(1)}, f32[96,1024]{1,0:T(8,128)S(1)}, u32[]{:S(2)}, u32[]{:S(2)}) collective-permute-start(f32[96,1024]{1,0:T(8,128)S(1)} %constant_dynamic-slice_fusion.4), channel_id=1, source_target_pairs={{0,2},{2,0},{4,6},{6,4},{8,10},{10,8},{12,14},{14,12},{1,3},{3,1},... | collective-permute-start | bytes 1179656 | tf_op jit(solution)/shard_map/ppermute | solution.py:55
  106.8 12.7 %collective-permute-start.12 = (bf16[192,1024]{1,0:T(8,128)(2,1)S(1)}, bf16[192,1024]{1,0:T(8,128)(2,1)S(1)}, u32[]{:S(2)}, u32[]{:S(2)}) collective-permute-start(bf16[192,1024]{1,0:T(8,128)(2,1)S(1)} %pad_maximum_fusion.3), channel_id=1, source_target_pairs={{0,2},{2,0},{4,6},{6,4},{8,10},{10,8},{12,14},{14,12},{1,3},{3,1},... | collective-permute-start | bytes 1179656 | tf_op jit(solution)/shard_map/ppermute | solution.py:35
  115.4 8.6 %collective-permute-start.3 = (f32[48,1024]{1,0:T(8,128)S(1)}, f32[48,1024]{1,0:T(8,128)S(1)}, u32[]{:S(2)}, u32[]{:S(2)}) collective-permute-start(f32[48,1024]{1,0:T(8,128)S(1)} %constant_dynamic-slice_fusion.3), channel_id=1, source_target_pairs={{0,32},{16,48},{32,0},{48,16},{64,96},{80,112},{96,64},{112,80},{1... | collective-permute-start | bytes 589832 | tf_op jit(solution)/shard_map/ppermute | solution.py:55
  119.8 18.8 %collective-permute-start.13 = (bf16[384,1024]{1,0:T(8,128)(2,1)S(1)}, bf16[384,1024]{1,0:T(8,128)(2,1)S(1)}, u32[]{:S(2)}, u32[]{:S(2)}) collective-permute-start(bf16[384,1024]{1,0:T(8,128)(2,1)S(1)} %pad_maximum_fusion.2), channel_id=1, source_target_pairs={{0,1},{1,0},{2,3},{3,2},{4,5},{5,4},{6,7},{7,6},{8,9},{9,8},{10,11... | collective-permute-start | bytes 2359304 | tf_op jit(solution)/shard_map/ppermute | solution.py:35
  124.1 8.3 %collective-permute-start.4 = (f32[24,1024]{1,0:T(8,128)S(1)}, f32[24,1024]{1,0:T(8,128)S(1)}, u32[]{:S(2)}, u32[]{:S(2)}) collective-permute-start(f32[24,1024]{1,0:T(8,128)S(1)} %constant_dynamic-slice_fusion.2), channel_id=1, source_target_pairs={{0,4},{2,6},{4,0},{6,2},{8,12},{10,14},{12,8},{14,10},{1,5},{3,7},... | collective-permute-start | bytes 294920 | tf_op jit(solution)/shard_map/ppermute | solution.py:55
  132.4 10.1 %collective-permute-start.5 = (f32[12,1024]{1,0:T(8,128)S(1)}, f32[12,1024]{1,0:T(8,128)S(1)}, u32[]{:S(2)}, u32[]{:S(2)}) collective-permute-start(f32[12,1024]{1,0:T(8,128)S(1)} %constant_dynamic-slice_fusion.1), channel_id=1, source_target_pairs={{0,64},{16,80},{32,96},{48,112},{64,0},{80,16},{96,32},{112,48},{1... | collective-permute-start | bytes 147464 | tf_op jit(solution)/shard_map/ppermute | solution.py:55
  142.6 9.7 %collective-permute-start.6 = (f32[6,1024]{1,0:T(8,128)S(1)}, f32[6,1024]{1,0:T(8,128)S(1)}, u32[]{:S(2)}, u32[]{:S(2)}) collective-permute-start(f32[6,1024]{1,0:T(8,128)S(1)} %constant_dynamic-slice_fusion), channel_id=1, source_target_pairs={{0,8},{2,10},{4,12},{6,14},{8,0},{10,2},{12,4},{14,6},{1,9},{3,11}... | collective-permute-start | bytes 73736 | tf_op jit(solution)/shard_map/ppermute | solution.py:55
  150.2 1.0 copy-start.2
  150.3 3.2 %copy-start.5 = (bf16[768,1024]{1,0:T(8,128)(2,1)}, bf16[768,1024]{1,0:T(8,128)(2,1)S(1)}, u32[]{:S(2)}) copy-start(bf16[768,1024]{1,0:T(8,128)(2,1)S(1)} %pad_maximum_fusion) | copy-start | bytes 4718596
  150.4 2.5 %copy-start.4 = (bf16[8,32,1792]{2,1,0:T(8,128)(2,1)S(1)}, bf16[8,32,1792]{2,1,0:T(8,128)(2,1)}, u32[]{:S(2)}) copy-start(bf16[8,32,1792]{2,1,0:T(8,128)(2,1)} %copy-done.3) | copy-start | bytes 2752516
  154.7 1.4 copy-start.6
  157.7 4.6 %copy-start.7 = (f32[6,1024]{1,0:T(8,128)S(1)}, f32[6,1024]{1,0:T(8,128)}, u32[]{:S(2)}) copy-start(f32[6,1024]{1,0:T(8,128)} %dynamic-slice_add_fusion.6) | copy-start | bytes 73732
  158.7 26.5 %all-to-all-start.1 = ((bf16[8,32,1792]{2,1,0:T(8,128)(2,1)}), bf16[8,32,1792]{2,1,0:T(8,128)(2,1)S(1)}, u32[]{:S(2)}, u32[]{:S(2)}) async-start(bf16[8,32,1792]{2,1,0:T(8,128)(2,1)} %pad_maximum_fusion.1), calls=%async_computation.1 | async-start | bytes 1835008 | tf_op jit(solution)/shard_map/all_to_all | solution.py:64

commit v6 on v4

--- a/solution.py
+++ b/solution.py
@@ -29,13 +29,11 @@
         .reshape(groups, CAP, ff + d)
     )
     weight = down_weight[0]
-    steps = (("y", 4), ("z", 4), ("y", 2), ("z", 2), ("y", 1), ("z", 1), ("c", 1))
-    for axis, bit in steps:
+    for axis, bit in (("z", 4), ("y", 4), ("z", 2), ("y", 2), ("z", 1), ("y", 1), ("c", 1)):
         n = lax.axis_size(axis)
         recv = lax.ppermute(weight, axis, [(i, i ^ bit) for i in range(n)])
         low = (lax.axis_index(axis) // bit) % 2 == 0
         weight = jnp.concatenate([jnp.where(low, weight, recv), jnp.where(low, recv, weight)], axis=0)
-    weight = weight.reshape(2, 2, 2, 2, 2, 2, 2, -1, d).transpose(6, 4, 2, 5, 3, 1, 0, 7, 8).reshape(ff, d)
     recv = lax.all_to_all(send, "expert", split_axis=0, concat_axis=0, tiled=True).reshape(width, ff + d)
     h_rows = recv[:, :ff]
     g_rows = recv[:, ff:]
@@ -51,10 +49,16 @@
         )
         summed = jnp.sum(parts, axis=0)
     summed, weight = lax.optimization_barrier((summed, weight))
-    y_rows = jnp.dot(h_rows, weight, preferred_element_type=jnp.float32).astype(jnp.bfloat16)
+    def order(x, axes):
+        return x.reshape((width,) + (2,) * 7 + (-1,)).transpose((0,) + axes + (8,)).reshape(width, ff)
+
+    y_rows = jnp.dot(
+        order(h_rows, (7, 3, 6, 2, 5, 1, 4)), weight, preferred_element_type=jnp.float32
+    ).astype(jnp.bfloat16)
     dh_rows = lax.dot_general(
         g_rows, weight, (((1,), (1,)), ((), ())), preferred_element_type=jnp.float32
     ).astype(jnp.bfloat16)
+    dh_rows = order(dh_rows, (6, 4, 2, 7, 5, 3, 1))
     back = lax.all_to_all(
         jnp.concatenate([y_rows, dh_rows], axis=1).reshape(groups, CAP, d + ff),
         "expert",

time: 182 us -> 187 us (1.027)
  other arithmetic: 8.42 us -> 13 us
  local copies, waits for them, and re-layouts: 9 us -> 6.8 us
    ppermute x7, waiting for transfers between devices: 48.9 us -> 41.2 us  [on_device(): recv = lax.ppermute(weight, axis, [(i, i ^ bit) for i in range(n)])]
    all_to_all x2, waiting for transfers between devices: 2.78 us -> 8.61 us  [on_device(): lax.all_to_all(summed.reshape(n, summed.shape[0] // n, d), axis, split_ax...]
    reshape x2 -> x3, local copies, waits for them, and re-layouts: 5.16 us -> 1.17 us  [order(): x.reshape((width,) + (2,) * 7 + (-1,)).transpose((0,) + axes + (8,))]
    all_to_all x1, waiting for transfers between devices: 23.4 us -> 25.8 us  [on_device(): lax.all_to_all(jnp.concatenate([y_rows, dh_rows], axis=1).reshape(groups,...]
    reduce_sum x3, other arithmetic: 1.7 us -> 3.93 us  [on_device(): summed = jnp.sum(parts, axis=0)]
    all_to_all x2, starting transfers between devices: 18.7 us -> 16.5 us  [on_device(): lax.all_to_all(summed.reshape(n, summed.shape[0] // n, d), axis, split_ax...]
    ppermute x7, starting transfers between devices: 41.6 us -> 43.6 us  [on_device(): recv = lax.ppermute(weight, axis, [(i, i ^ bit) for i in range(n)])]
  transfers between devices with their start and end apart: 11 -> 11, of which waited for: 7 -> 7; matrix products, arithmetic and copies ran while one was open for 8% -> 7% of each run, Pallas kernels for 0% -> 0%
where the time goes in v6:
time: 187 us; the launch traced here: 185 us
  waiting for transfers between devices  75.6 us (40%)
  starting transfers between devices  72.8 us (39%)
  other arithmetic  13 us (7%)
  blocking collectives  8.57 us (5%)
  matrix products  7 us (4%)
  local copies, waits for them, and re-layouts  6.8 us (4%)
    ppermute x7, starting transfers between devices, on_device(): recv = lax.ppermute(weight, axis, [(i, i ^ bit) for i in range(n)])  43.6 us
    ppermute x7, waiting for transfers between devices, on_device(): recv = lax.ppermute(weight, axis, [(i, i ^ bit) for i in range(n)])  41.2 us
    all_to_all x1, waiting for transfers between devices, on_device(): lax.all_to_all(jnp.concatenate([y_rows, dh_rows], axis=1).reshape(groups,...  25.8 us
    all_to_all x2, starting transfers between devices, on_device(): lax.all_to_all(summed.reshape(n, summed.shape[0] // n, d), axis, split_ax...  16.5 us
    all_to_all x2, waiting for transfers between devices, on_device(): lax.all_to_all(summed.reshape(n, summed.shape[0] // n, d), axis, split_ax...  8.61 us
    all_to_all x1, blocking collectives, on_device(): lax.all_to_all(summed.reshape(n, summed.shape[0] // n, d), axis, split_ax...  8.57 us
    all_to_all x1, starting transfers between devices, on_device(): lax.all_to_all(send, 'expert', split_axis=0, concat_axis=0, tiled=True)  7.31 us
    all_to_all x1, starting transfers between devices, on_device(): lax.all_to_all(jnp.concatenate([y_rows, dh_rows], axis=1).reshape(groups,...  5.4 us
  transfers between devices with their start and end apart: 11, of which 7 were waited for; matrix products, arithmetic and copies ran while one was open for 7% of the time, Pallas kernels for 0%

profile of v6, /device:TPU:1, one launch (start us, length us, event | category | flops | bytes accessed | tf_op | source)
XLA Modules:
  0.0 185.5 jit_solution(1048371634204254014)
XLA Ops:
  3.7 2.3 %convolution_convert_fusion = bf16[256,1792]{1,0:T(8,128)(2,1)} fusion(bf16[128,1024]{1,0:T(8,128)(2,1)} %param.6, bf16[128,768]{1,0:T(8,128)(2,1)} %param.5, s32[128]{0:T(128)S(1)} %multiply_add_fusion, pred[128]{0:T(512)(128)(4,1)S(1)} %iota_compare_fusion.2), kind=kOutput, calls=%fused_computation | convolution fusion | flops 118882304 | bytes 1376896 | tf_op jit(solution)/shard_map/dot_general | solution.py:27
  6.0 7.3 %all-to-all-start = ((bf16[8,32,1792]{2,1,0:T(8,128)(2,1)}), bf16[8,32,1792]{2,1,0:T(8,128)(2,1)S(1)}, u32[]{:S(2)}, u32[]{:S(2)}) async-start(bf16[8,32,1792]{2,1,0:T(8,128)(2,1)} %bitcast.2), calls=%async_computation | async-start | bytes 1835008 | tf_op jit(solution)/shard_map/all_to_all | solution.py:37
  13.4 14.3 %collective-permute-start = (bf16[6,1024]{1,0:T(8,128)(2,1)S(1)}, bf16[6,1024]{1,0:T(8,128)(2,1)S(1)}, u32[]{:S(2)}, u32[]{:S(2)}) collective-permute-start(bf16[6,1024]{1,0:T(8,128)(2,1)S(1)} %bitcast.48), channel_id=1, source_target_pairs={{0,8},{2,10},{4,12},{6,14},{8,0},{10,2},{12,4},{14,6},{1,9},{3,11}... | collective-permute-start | bytes 36872 | tf_op jit(solution)/shard_map/ppermute | solution.py:34
  27.7 1.1 collective-permute-done
  28.8 7.9 %collective-permute-start.1 = (bf16[12,1024]{1,0:T(8,128)(2,1)S(1)}, bf16[12,1024]{1,0:T(8,128)(2,1)S(1)}, u32[]{:S(2)}, u32[]{:S(2)}) collective-permute-start(bf16[12,1024]{1,0:T(8,128)(2,1)S(1)} %pad_maximum_fusion.7), channel_id=1, source_target_pairs={{0,64},{16,80},{32,96},{48,112},{64,0},{80,16},{96,32},{112,48},{1... | collective-permute-start | bytes 73736 | tf_op jit(solution)/shard_map/ppermute | solution.py:34
  36.8 1.3 collective-permute-done.1
  38.8 6.0 %collective-permute-start.2 = (bf16[24,1024]{1,0:T(8,128)(2,1)}, bf16[24,1024]{1,0:T(8,128)(2,1)}, u32[]{:S(2)}, u32[]{:S(2)}) collective-permute-start(bf16[24,1024]{1,0:T(8,128)(2,1)} %pad_maximum_fusion.6), channel_id=1, source_target_pairs={{0,4},{2,6},{4,0},{6,2},{8,12},{10,14},{12,8},{14,10},{1,5},{3,7},... | collective-permute-start | bytes 147464 | tf_op jit(solution)/shard_map/ppermute | solution.py:34
  46.3 8.6 %all_to_all.25 = f32[2,384,1024]{2,1,0:T(8,128)S(1)} all-to-all(f32[2,384,1024]{2,1,0:T(8,128)S(1)} %fusion.1), channel_id=1, replica_groups=mesh['expert'=8,'y'=8,'z'=8,'c'=2] {'c'}, dimensions={0} | all-to-all | bytes 6291456 | tf_op jit(solution)/shard_map/all_to_all | solution.py:47
  54.9 1.6 reduce_sum.37
  56.5 9.2 %all-to-all-start.2 = ((f32[8,48,1024]{2,1,0:T(8,128)}), f32[8,48,1024]{2,1,0:T(8,128)S(1)}, u32[]{:S(2)}, u32[]{:S(2)}) async-start(f32[8,48,1024]{2,1,0:T(8,128)} %bitcast.37), calls=%async_computation.2 | async-start | bytes 3145728 | tf_op jit(solution)/shard_map/all_to_all | solution.py:47
  66.6 4.4 %collective-permute-start.3 = (bf16[48,1024]{1,0:T(8,128)(2,1)S(1)}, bf16[48,1024]{1,0:T(8,128)(2,1)S(1)}, u32[]{:S(2)}, u32[]{:S(2)}) collective-permute-start(bf16[48,1024]{1,0:T(8,128)(2,1)S(1)} %pad_maximum_fusion.5), channel_id=1, source_target_pairs={{0,32},{16,48},{32,0},{48,16},{64,96},{80,112},{96,64},{112,80},{1... | collective-permute-start | bytes 294920 | tf_op jit(solution)/shard_map/ppermute | solution.py:34
  71.1 2.4 %collective-permute-done.3 = bf16[48,1024]{1,0:T(8,128)(2,1)S(1)} collective-permute-done((bf16[48,1024]{1,0:T(8,128)(2,1)S(1)}, bf16[48,1024]{1,0:T(8,128)(2,1)S(1)}, u32[]{:S(2)}, u32[]{:S(2)}) %collective-permute-start.3) | collective-permute-done | bytes 98336 | tf_op jit(solution)/shard_map/ppermute | solution.py:34
  73.6 3.2 %collective-permute-start.4 = (bf16[96,1024]{1,0:T(8,128)(2,1)S(1)}, bf16[96,1024]{1,0:T(8,128)(2,1)S(1)}, u32[]{:S(2)}, u32[]{:S(2)}) collective-permute-start(bf16[96,1024]{1,0:T(8,128)(2,1)S(1)} %pad_maximum_fusion.4), channel_id=1, source_target_pairs={{0,2},{2,0},{4,6},{6,4},{8,10},{10,8},{12,14},{14,12},{1,3},{3,1},... | collective-permute-start | bytes 589832 | tf_op jit(solution)/shard_map/ppermute | solution.py:34
  76.8 28.6 %collective-permute-done.4 = bf16[96,1024]{1,0:T(8,128)(2,1)S(1)} collective-permute-done((bf16[96,1024]{1,0:T(8,128)(2,1)S(1)}, bf16[96,1024]{1,0:T(8,128)(2,1)S(1)}, u32[]{:S(2)}, u32[]{:S(2)}) %collective-permute-start.4) | collective-permute-done | bytes 196640 | tf_op jit(solution)/shard_map/ppermute | solution.py:34
  105.5 3.3 %collective-permute-start.5 = (bf16[192,1024]{1,0:T(8,128)(2,1)S(1)}, bf16[192,1024]{1,0:T(8,128)(2,1)}, u32[]{:S(2)}, u32[]{:S(2)}) collective-permute-start(bf16[192,1024]{1,0:T(8,128)(2,1)S(1)} %pad_maximum_fusion.3), channel_id=1, source_target_pairs={{0,16},{16,0},{32,48},{48,32},{64,80},{80,64},{96,112},{112,96},{1... | collective-permute-start | bytes 1179656 | tf_op jit(solution)/shard_map/ppermute | solution.py:34
  108.9 7.7 %collective-permute-done.5 = bf16[192,1024]{1,0:T(8,128)(2,1)} collective-permute-done((bf16[192,1024]{1,0:T(8,128)(2,1)S(1)}, bf16[192,1024]{1,0:T(8,128)(2,1)}, u32[]{:S(2)}, u32[]{:S(2)}) %collective-permute-start.5) | collective-permute-done | bytes 393248 | tf_op jit(solution)/shard_map/ppermute | solution.py:34
  116.6 1.2 broadcast_select_fusion.3
  117.9 4.4 %collective-permute-start.6 = (bf16[384,1024]{1,0:T(8,128)(2,1)S(1)}, bf16[384,1024]{1,0:T(8,128)(2,1)}, u32[]{:S(2)}, u32[]{:S(2)}) collective-permute-start(bf16[384,1024]{1,0:T(8,128)(2,1)S(1)} %pad_maximum_fusion.2), channel_id=1, source_target_pairs={{0,1},{1,0},{2,3},{3,2},{4,5},{5,4},{6,7},{7,6},{8,9},{9,8},{10,11... | collective-permute-start | bytes 2359304 | tf_op jit(solution)/shard_map/ppermute | solution.py:34
  123.0 1.7 reshape.62
  124.7 7.3 %all-to-all-start.3 = ((f32[8,6,1024]{2,1,0:T(8,128)}), f32[8,6,1024]{2,1,0:T(8,128)}, u32[]{:S(2)}, u32[]{:S(2)}) async-start(f32[8,6,1024]{2,1,0:T(8,128)} %reshape.62), calls=%async_computation.3 | async-start | bytes 524288 | tf_op jit(solution)/shard_map/all_to_all | solution.py:47
  132.0 1.5 broadcast_select_fusion.1
  133.4 1.3 pad_maximum_fusion
  134.9 0.9 reshape.58
  135.8 8.6 %all-to-all-done.3 = f32[8,6,1024]{2,1,0:T(8,128)} async-done(((f32[8,6,1024]{2,1,0:T(8,128)}), f32[8,6,1024]{2,1,0:T(8,128)}, u32[]{:S(2)}, u32[]{:S(2)}) %all-to-all-start.3) | async-done | bytes 196640 | tf_op jit(solution)/shard_map/all_to_all | solution.py:47
  144.4 1.6 reduce_sum.39
  147.8 1.0 copy.22
  149.2 1.6 convolution_convert_fusion.1
  150.8 1.0 pad_maximum_fusion.1
  151.8 5.4 %all-to-all-start.4 = ((bf16[8,32,1792]{2,1,0:T(8,128)(2,1)}), bf16[8,32,1792]{2,1,0:T(8,128)(2,1)S(1)}, u32[]{:S(2)}, u32[]{:S(2)}) async-start(bf16[8,32,1792]{2,1,0:T(8,128)(2,1)} %pad_maximum_fusion.1), calls=%async_computation.4 | async-start | bytes 1835008 | tf_op jit(solution)/shard_map/all_to_all | solution.py:62
  157.8 25.8 %all-to-all-done.4 = bf16[8,32,1792]{2,1,0:T(8,128)(2,1)S(1)} async-done(((bf16[8,32,1792]{2,1,0:T(8,128)(2,1)}), bf16[8,32,1792]{2,1,0:T(8,128)(2,1)S(1)}, u32[]{:S(2)}, u32[]{:S(2)}) %all-to-all-start.4) | async-done | bytes 917536 | tf_op jit(solution)/shard_map/all_to_all | solution.py:62
  183.6 1.0 convolution_convert_fusion.3
  184.6 0.9 convolution_convert_fusion.4
  (55 shorter events, 9.4 us)
Async XLA Ops:
  3.7 9.6 %copy-start.9 = (bf16[1,6,1024]{2,1,0:T(8,128)(2,1)S(1)}, bf16[1,6,1024]{2,1,0:T(8,128)(2,1)}, u32[]{:S(2)}) copy-start(bf16[1,6,1024]{2,1,0:T(8,128)(2,1)} %param.9) | copy-start | bytes 36868
  6.0 38.8 %all-to-all-start = ((bf16[8,32,1792]{2,1,0:T(8,128)(2,1)}), bf16[8,32,1792]{2,1,0:T(8,128)(2,1)S(1)}, u32[]{:S(2)}, u32[]{:S(2)}) async-start(bf16[8,32,1792]{2,1,0:T(8,128)(2,1)} %bitcast.2), calls=%async_computation | async-start | bytes 1835008 | tf_op jit(solution)/shard_map/all_to_all | solution.py:37
  13.4 15.4 %collective-permute-start = (bf16[6,1024]{1,0:T(8,128)(2,1)S(1)}, bf16[6,1024]{1,0:T(8,128)(2,1)S(1)}, u32[]{:S(2)}, u32[]{:S(2)}) collective-permute-start(bf16[6,1024]{1,0:T(8,128)(2,1)S(1)} %bitcast.48), channel_id=1, source_target_pairs={{0,8},{2,10},{4,12},{6,14},{8,0},{10,2},{12,4},{14,6},{1,9},{3,11}... | collective-permute-start | bytes 36872 | tf_op jit(solution)/shard_map/ppermute | solution.py:34
  28.8 9.3 %collective-permute-start.1 = (bf16[12,1024]{1,0:T(8,128)(2,1)S(1)}, bf16[12,1024]{1,0:T(8,128)(2,1)S(1)}, u32[]{:S(2)}, u32[]{:S(2)}) collective-permute-start(bf16[12,1024]{1,0:T(8,128)(2,1)S(1)} %pad_maximum_fusion.7), channel_id=1, source_target_pairs={{0,64},{16,80},{32,96},{48,112},{64,0},{80,16},{96,32},{112,48},{1... | collective-permute-start | bytes 73736 | tf_op jit(solution)/shard_map/ppermute | solution.py:34
  38.1 0.7 copy-start.4
  38.1 0.7 copy-start.6
  38.8 26.9 %collective-permute-start.2 = (bf16[24,1024]{1,0:T(8,128)(2,1)}, bf16[24,1024]{1,0:T(8,128)(2,1)}, u32[]{:S(2)}, u32[]{:S(2)}) collective-permute-start(bf16[24,1024]{1,0:T(8,128)(2,1)} %pad_maximum_fusion.6), channel_id=1, source_target_pairs={{0,4},{2,6},{4,0},{6,2},{8,12},{10,14},{12,8},{14,10},{1,5},{3,7},... | collective-permute-start | bytes 147464 | tf_op jit(solution)/shard_map/ppermute | solution.py:34
  44.8 0.9 copy-start
  56.5 9.3 %copy-start.5 = (bf16[12,1024]{1,0:T(8,128)(2,1)S(1)}, bf16[12,1024]{1,0:T(8,128)(2,1)}, u32[]{:S(2)}) copy-start(bf16[12,1024]{1,0:T(8,128)(2,1)} %copy-done.4) | copy-start | bytes 73732
  56.5 9.3 %copy-start.7 = (bf16[12,1024]{1,0:T(8,128)(2,1)S(1)}, bf16[12,1024]{1,0:T(8,128)(2,1)}, u32[]{:S(2)}) copy-start(bf16[12,1024]{1,0:T(8,128)(2,1)} %copy-done.6) | copy-start | bytes 73732
  56.5 65.8 %all-to-all-start.2 = ((f32[8,48,1024]{2,1,0:T(8,128)}), f32[8,48,1024]{2,1,0:T(8,128)S(1)}, u32[]{:S(2)}, u32[]{:S(2)}) async-start(f32[8,48,1024]{2,1,0:T(8,128)} %bitcast.37), calls=%async_computation.2 | async-start | bytes 3145728 | tf_op jit(solution)/shard_map/all_to_all | solution.py:47
  66.6 6.9 %collective-permute-start.3 = (bf16[48,1024]{1,0:T(8,128)(2,1)S(1)}, bf16[48,1024]{1,0:T(8,128)(2,1)S(1)}, u32[]{:S(2)}, u32[]{:S(2)}) collective-permute-start(bf16[48,1024]{1,0:T(8,128)(2,1)S(1)} %pad_maximum_fusion.5), channel_id=1, source_target_pairs={{0,32},{16,48},{32,0},{48,16},{64,96},{80,112},{96,64},{112,80},{1... | collective-permute-start | bytes 294920 | tf_op jit(solution)/shard_map/ppermute | solution.py:34
  73.6 31.9 %collective-permute-start.4 = (bf16[96,1024]{1,0:T(8,128)(2,1)S(1)}, bf16[96,1024]{1,0:T(8,128)(2,1)S(1)}, u32[]{:S(2)}, u32[]{:S(2)}) collective-permute-start(bf16[96,1024]{1,0:T(8,128)(2,1)S(1)} %pad_maximum_fusion.4), channel_id=1, source_target_pairs={{0,2},{2,0},{4,6},{6,4},{8,10},{10,8},{12,14},{14,12},{1,3},{3,1},... | collective-permute-start | bytes 589832 | tf_op jit(solution)/shard_map/ppermute | solution.py:34
  105.5 11.1 %collective-permute-start.5 = (bf16[192,1024]{1,0:T(8,128)(2,1)S(1)}, bf16[192,1024]{1,0:T(8,128)(2,1)}, u32[]{:S(2)}, u32[]{:S(2)}) collective-permute-start(bf16[192,1024]{1,0:T(8,128)(2,1)S(1)} %pad_maximum_fusion.3), channel_id=1, source_target_pairs={{0,16},{16,0},{32,48},{48,32},{64,80},{80,64},{96,112},{112,96},{1... | collective-permute-start | bytes 1179656 | tf_op jit(solution)/shard_map/ppermute | solution.py:34
  117.9 14.1 %collective-permute-start.6 = (bf16[384,1024]{1,0:T(8,128)(2,1)S(1)}, bf16[384,1024]{1,0:T(8,128)(2,1)}, u32[]{:S(2)}, u32[]{:S(2)}) collective-permute-start(bf16[384,1024]{1,0:T(8,128)(2,1)S(1)} %pad_maximum_fusion.2), channel_id=1, source_target_pairs={{0,1},{1,0},{2,3},{3,2},{4,5},{5,4},{6,7},{7,6},{8,9},{9,8},{10,11... | collective-permute-start | bytes 2359304 | tf_op jit(solution)/shard_map/ppermute | solution.py:34
  124.7 19.8 %all-to-all-start.3 = ((f32[8,6,1024]{2,1,0:T(8,128)}), f32[8,6,1024]{2,1,0:T(8,128)}, u32[]{:S(2)}, u32[]{:S(2)}) async-start(f32[8,6,1024]{2,1,0:T(8,128)} %reshape.62), calls=%async_computation.3 | async-start | bytes 524288 | tf_op jit(solution)/shard_map/all_to_all | solution.py:47
  134.7 11.3 %copy-start.1 = (bf16[8,32,1792]{2,1,0:T(8,128)(2,1)S(1)}, bf16[8,32,1792]{2,1,0:T(8,128)(2,1)}, u32[]{:S(2)}) copy-start(bf16[8,32,1792]{2,1,0:T(8,128)(2,1)} %copy-done) | copy-start | bytes 2752516
  134.9 11.2 %copy-start.2 = (bf16[768,1024]{1,0:T(8,128)(2,1)S(1)}, bf16[768,1024]{1,0:T(8,128)(2,1)}, u32[]{:S(2)}) copy-start(bf16[768,1024]{1,0:T(8,128)(2,1)} %pad_maximum_fusion) | copy-start | bytes 4718596
  147.8 1.4 copy-start.3
  150.8 6.4 %copy-start.8 = (f32[6,1024]{1,0:T(8,128)S(1)}, f32[6,1024]{1,0:T(8,128)}, u32[]{:S(2)}) copy-start(f32[6,1024]{1,0:T(8,128)} %reduce_sum.39) | copy-start | bytes 73732
  151.8 31.8 %all-to-all-start.4 = ((bf16[8,32,1792]{2,1,0:T(8,128)(2,1)}), bf16[8,32,1792]{2,1,0:T(8,128)(2,1)S(1)}, u32[]{:S(2)}, u32[]{:S(2)}) async-start(bf16[8,32,1792]{2,1,0:T(8,128)(2,1)} %pad_maximum_fusion.1), calls=%async_computation.4 | async-start | bytes 1835008 | tf_op jit(solution)/shard_map/all_to_all | solution.py:62

commit v7 on v3

--- a/solution.py
+++ b/solution.py
@@ -28,7 +28,7 @@
         .astype(jnp.bfloat16)
         .reshape(groups, CAP, ff + d)
     )
-    weight = lax.all_gather(down_weight, DP, axis=1, tiled=True)[0]
+    weight = lax.all_gather(down_weight.reshape(1, -1), DP, axis=0, tiled=True).reshape(ff, d)
     recv = lax.all_to_all(send, "expert", split_axis=0, concat_axis=0, tiled=True).reshape(width, ff + d)
     h_rows = recv[:, :ff]
     g_rows = recv[:, ff:]

time: 179 us -> 191 us (1.067)
  other arithmetic: 5.05 us -> 15.7 us
    all_gather x0 -> x1, other arithmetic: none -> 10.6 us  [on_device(): lax.all_gather(down_weight.reshape(1, -1), DP, axis=0, tiled=True)]
    unnamed x8 -> x9, local copies, waits for them, and re-layouts: 3.52 us -> 1.05 us
    reshape x0 -> x1, local copies, waits for them, and re-layouts: none -> 2.38 us  [on_device(): lax.all_gather(down_weight.reshape(1, -1), DP, axis=0, tiled=True)]
  transfers between devices with their start and end apart: 4 -> 4, of which waited for: 3 -> 3; matrix products, arithmetic and copies ran while one was open for 4% -> 9% of each run, Pallas kernels for 0% -> 0%
where the time goes in v7:
time: 191 us
  blocking collectives  74.4 us (39%)
  waiting for transfers between devices  53.5 us (28%)
  starting transfers between devices  19.7 us (10%)
  other arithmetic  15.7 us (8%)
  between operations  14.8 us (8%)
  matrix products  7.51 us (4%)
  local copies, waits for them, and re-layouts  5.29 us (3%)
    all_to_all x2, blocking collectives, on_device(): lax.all_to_all(summed.reshape(n, summed.shape[0] // n, d), axis, split_ax...  74.4 us
    all_to_all x1, waiting for transfers between devices, on_device(): lax.all_to_all(jnp.concatenate([y_rows, dh_rows], axis=1).reshape(groups,...  25.8 us
    all_to_all x1, waiting for transfers between devices, on_device(): lax.all_to_all(send, 'expert', split_axis=0, concat_axis=0, tiled=True)  15.8 us
    all_gather x1, waiting for transfers between devices, on_device(): lax.all_gather(down_weight.reshape(1, -1), DP, axis=0, tiled=True)  11.9 us
    all_gather x1, other arithmetic, on_device(): lax.all_gather(down_weight.reshape(1, -1), DP, axis=0, tiled=True)  10.6 us
    all_to_all x1, starting transfers between devices, on_device(): lax.all_to_all(summed.reshape(n, summed.shape[0] // n, d), axis, split_ax...  7.7 us
    all_to_all x1, starting transfers between devices, on_device(): lax.all_to_all(send, 'expert', split_axis=0, concat_axis=0, tiled=True)  7.31 us
    all_to_all x1, starting transfers between devices, on_device(): lax.all_to_all(jnp.concatenate([y_rows, dh_rows], axis=1).reshape(groups,...  4.68 us
  transfers between devices with their start and end apart: 4, of which 3 were waited for; matrix products, arithmetic and copies ran while one was open for 9% of the time, Pallas kernels for 0%

profile of v7, /device:TPU:1, one launch (start us, length us, event | category | flops | bytes accessed | tf_op | source)
XLA Modules:
  0.0 190.9 jit_solution(13474124516741612337)
XLA Ops:
  7.2 0.7 fusion.16
  7.9 0.2 reduce_window_sum.11
  8.1 0.8 select_reduce_fusion
  8.9 0.7 multiply_add_fusion
  10.3 2.3 %convolution_convert_fusion = bf16[256,1792]{1,0:T(8,128)(2,1)} fusion(bf16[128,1024]{1,0:T(8,128)(2,1)} %param.6, bf16[128,768]{1,0:T(8,128)(2,1)} %param.5, s32[128]{0:T(128)S(1)} %multiply_add_fusion, pred[128]{0:T(512)(128)(4,1)S(1)} %iota_compare_fusion.2), kind=kOutput, calls=%fused_computation | convolution fusion | flops 118882304 | bytes 1376896 | tf_op jit(solution)/shard_map/dot_general | solution.py:27
  12.6 7.3 %all-to-all-start = ((bf16[8,32,1792]{2,1,0:T(8,128)(2,1)}), bf16[8,32,1792]{2,1,0:T(8,128)(2,1)S(1)}, u32[]{:S(2)}, u32[]{:S(2)}) async-start(bf16[8,32,1792]{2,1,0:T(8,128)(2,1)} %bitcast.2), calls=%async_computation | async-start | bytes 1835008 | tf_op jit(solution)/shard_map/all_to_all | solution.py:32
  19.9 0.0 all-gather.3.cloned.1.call-start
  19.9 0.6 reshape.60
  20.6 0.0 all-gather.3.cloned.1.call-update
  20.6 15.8 %all-to-all-done = bf16[8,32,1792]{2,1,0:T(8,128)(2,1)S(1)} async-done(((bf16[8,32,1792]{2,1,0:T(8,128)(2,1)}), bf16[8,32,1792]{2,1,0:T(8,128)(2,1)S(1)}, u32[]{:S(2)}, u32[]{:S(2)}) %all-to-all-start) | async-done | bytes 917536 | tf_op jit(solution)/shard_map/all_to_all | solution.py:32
  36.4 0.2 copy.13
  36.6 0.1 reshape.52
  36.8 0.1 reshape.53
  36.9 0.4 copy-done
  37.3 0.6 fusion.1
  37.9 17.2 %all_to_all.25 = f32[2,384,1024]{2,1,0:T(8,128)S(1)} all-to-all(f32[2,384,1024]{2,1,0:T(8,128)S(1)} %fusion.1), channel_id=1, replica_groups=mesh['expert'=8,'y'=8,'z'=8,'c'=2] {'c'}, dimensions={0} | all-to-all | bytes 6291456 | tf_op jit(solution)/shard_map/all_to_all | solution.py:42
  55.1 1.5 reduce_sum.37
  56.6 57.2 %all_to_all.26 = f32[8,48,1024]{2,1,0:T(8,128)S(1)} all-to-all(f32[8,48,1024]{2,1,0:T(8,128)} %bitcast.23), channel_id=1, replica_groups=mesh['expert'=8,'y'=8,'z'=8,'c'=2] {'z'}, dimensions={0} | all-to-all | bytes 3145728 | tf_op jit(solution)/shard_map/all_to_all | solution.py:42
  113.9 0.1 reduce_sum.38
  114.0 0.7 reshape.55
  114.7 7.7 %all-to-all-start.3 = ((f32[8,6,1024]{2,1,0:T(8,128)}), f32[8,6,1024]{2,1,0:T(8,128)S(1)}, u32[]{:S(2)}, u32[]{:S(2)}) async-start(f32[8,6,1024]{2,1,0:T(8,128)} %reshape.55), calls=%async_computation.3 | async-start | bytes 524288 | tf_op jit(solution)/shard_map/all_to_all | solution.py:42
  122.4 11.9 %all-gather.3.cloned.1.call-done = bf16[128,1,6144]{2,1,0:T(2,128)(2,1)} async-done(((bf16[1,1,6144]{2,1,0:T(2,128)(2,1)}), bf16[128,1,6144]{2,1,0:T(2,128)(2,1)}) %all-gather.3.cloned.1.call-update) | async-done | bytes 1572880 | tf_op jit(solution)/shard_map/all_gather | solution.py:31
  134.3 10.6 %reduce = bf16[128,6144]{1,0:T(8,128)(2,1)S(1)} reduce(bf16[128,1,6144]{2,1,0:T(2,128)(2,1)} %all-gather.3.cloned.1.call-done, bf16[]{:T(256)} %constant.18), dimensions={1}, to_apply=%all-gather.reduce_sub_computation | reduce | bytes 3145730 | tf_op jit(solution)/shard_map/all_gather | solution.py:31
  144.9 2.4 %reshape.57 = bf16[768,1024]{1,0:T(8,128)(2,1)} reshape(bf16[128,6144]{1,0:T(8,128)(2,1)S(1)} %reduce) | data formatting | bytes 3145728 | tf_op jit(solution)/shard_map/reshape | solution.py:31
  147.3 2.1 %convolution_convert_fusion.1 = bf16[256,1024]{1,0:T(8,128)(2,1)S(1)} fusion(bf16[768,1024]{1,0:T(8,128)(2,1)} %reshape.57, bf16[256,1792]{1,0:T(8,128)(2,1)S(1)} %bitcast.28), kind=kOutput, calls=%fused_computation.1 | convolution fusion | flops 402915328 | bytes 2490368 | tf_op jit(solution)/shard_map/dot_general | solution.py:47
  149.4 0.6 convolution_convert_fusion.2
  150.1 1.0 pad_maximum_fusion
  151.0 4.7 %all-to-all-start.4 = ((bf16[8,32,1792]{2,1,0:T(8,128)(2,1)}), bf16[8,32,1792]{2,1,0:T(8,128)(2,1)S(1)}, u32[]{:S(2)}, u32[]{:S(2)}) async-start(bf16[8,32,1792]{2,1,0:T(8,128)(2,1)} %bitcast.9), calls=%async_computation.4 | async-start | bytes 1835008 | tf_op jit(solution)/shard_map/all_to_all | solution.py:51
  155.7 0.6 broadcast_in_dim.2
  156.4 25.8 %all-to-all-done.4 = bf16[8,32,1792]{2,1,0:T(8,128)(2,1)S(1)} async-done(((bf16[8,32,1792]{2,1,0:T(8,128)(2,1)}), bf16[8,32,1792]{2,1,0:T(8,128)(2,1)S(1)}, u32[]{:S(2)}, u32[]{:S(2)}) %all-to-all-start.4) | async-done | bytes 917536 | tf_op jit(solution)/shard_map/all_to_all | solution.py:51
  182.1 0.9 convolution_convert_fusion.4
  183.0 1.0 convolution_convert_fusion.3
  (12 shorter events, 0.1 us)
Async XLA Ops:
  10.2 9.7 %copy-start.3 = (bf16[1,6,1024]{2,1,0:T(8,128)(2,1)S(1)}, bf16[1,6,1024]{2,1,0:T(8,128)(2,1)}, u32[]{:S(2)}) copy-start(bf16[1,6,1024]{2,1,0:T(8,128)(2,1)} %param.9) | copy-start | bytes 36868
  12.6 23.8 %all-to-all-start = ((bf16[8,32,1792]{2,1,0:T(8,128)(2,1)}), bf16[8,32,1792]{2,1,0:T(8,128)(2,1)S(1)}, u32[]{:S(2)}, u32[]{:S(2)}) async-start(bf16[8,32,1792]{2,1,0:T(8,128)(2,1)} %bitcast.2), calls=%async_computation | async-start | bytes 1835008 | tf_op jit(solution)/shard_map/all_to_all | solution.py:32
  19.9 114.4 %all-gather.3.cloned.1.call-start = ((), (), s32[]{:S(2)}) async-start(), calls=%async_computation.5 | async-start | bytes 3170304 | tf_op jit(solution)/shard_map/all_gather | solution.py:31
  36.4 0.9 copy-start
  114.7 32.6 %all-to-all-start.3 = ((f32[8,6,1024]{2,1,0:T(8,128)}), f32[8,6,1024]{2,1,0:T(8,128)S(1)}, u32[]{:S(2)}, u32[]{:S(2)}) async-start(f32[8,6,1024]{2,1,0:T(8,128)} %reshape.55), calls=%async_computation.3 | async-start | bytes 524288 | tf_op jit(solution)/shard_map/all_to_all | solution.py:42
  144.9 2.4 %copy-start.1 = (bf16[8,32,1792]{2,1,0:T(8,128)(2,1)S(1)}, bf16[8,32,1792]{2,1,0:T(8,128)(2,1)}, u32[]{:S(2)}) copy-start(bf16[8,32,1792]{2,1,0:T(8,128)(2,1)} %copy-done) | copy-start | bytes 2752516
  147.3 2.1 %copy-start.2 = (bf16[768,1024]{1,0:T(8,128)(2,1)S(1)}, bf16[768,1024]{1,0:T(8,128)(2,1)}, u32[]{:S(2)}) copy-start(bf16[768,1024]{1,0:T(8,128)(2,1)} %reshape.57) | copy-start | bytes 4718596
  151.0 31.1 %all-to-all-start.4 = ((bf16[8,32,1792]{2,1,0:T(8,128)(2,1)}), bf16[8,32,1792]{2,1,0:T(8,128)(2,1)S(1)}, u32[]{:S(2)}, u32[]{:S(2)}) async-start(bf16[8,32,1792]{2,1,0:T(8,128)(2,1)} %bitcast.9), calls=%async_computation.4 | async-start | bytes 1835008 | tf_op jit(solution)/shard_map/all_to_all | solution.py:51
Sparse Core Ops, SparseCore 0:
  25.6 108.6 all-gather.2

commit v8 on v3

--- a/solution.py
+++ b/solution.py
@@ -16,8 +16,9 @@
     width = groups * CAP
     ids = expert_ids[:, 0]
     live = jnp.arange(tok_rows, dtype=jnp.int32) < counts[0, 0]
-    member = (ids[:, None] == jnp.arange(groups, dtype=jnp.int32)[None, :]).astype(jnp.int32)
-    rank = jnp.sum((jnp.cumsum(member, 0) - 1) * member, 1)
+    slots = jnp.arange(tok_rows, dtype=jnp.int32)
+    earlier = jnp.logical_and(ids[:, None] == ids[None, :], slots[None, :] < slots[:, None])
+    rank = jnp.sum(earlier.astype(jnp.int32), 1)
     target = ids * CAP + rank
     placing = jnp.logical_and(
         target[None, :] == jnp.arange(width, dtype=jnp.int32)[:, None], live[None, :]

time: 179 us -> 179 us (level)
  no operation moved by 1% of the time
where the time goes in v8:
time: 179 us; the launch traced here: 178 us
  blocking collectives  74.4 us (42%)
  waiting for transfers between devices  53.8 us (30%)
  starting transfers between devices  19.4 us (11%)
  between operations  14.8 us (8%)
  matrix products  6.01 us (3%)
  local copies, waits for them, and re-layouts  5.4 us (3%)
  other arithmetic  4.24 us (2%)
    all_to_all x2, blocking collectives, on_device(): lax.all_to_all(summed.reshape(n, summed.shape[0] // n, d), axis, split_ax...  74.4 us
    all_to_all x1, waiting for transfers between devices, on_device(): lax.all_to_all(jnp.concatenate([y_rows, dh_rows], axis=1).reshape(groups,...  25.8 us
    all_to_all x1, waiting for transfers between devices, on_device(): lax.all_to_all(send, 'expert', split_axis=0, concat_axis=0, tiled=True)  15.8 us
    all_gather x1, waiting for transfers between devices, on_device(): weight = lax.all_gather(down_weight, DP, axis=1, tiled=True)[0]  12.2 us
    all_to_all x1, starting transfers between devices, on_device(): lax.all_to_all(summed.reshape(n, summed.shape[0] // n, d), axis, split_ax...  7.51 us
    all_to_all x1, starting transfers between devices, on_device(): lax.all_to_all(send, 'expert', split_axis=0, concat_axis=0, tiled=True)  7.31 us
    all_to_all x1, starting transfers between devices, on_device(): lax.all_to_all(jnp.concatenate([y_rows, dh_rows], axis=1).reshape(groups,...  4.53 us
  transfers between devices with their start and end apart: 4, of which 3 were waited for; matrix products, arithmetic and copies ran while one was open for 4% of the time, Pallas kernels for 0%

profile of v8, /device:TPU:1, one launch (start us, length us, event | category | flops | bytes accessed | tf_op | source)
XLA Modules:
  0.0 178.0 jit_solution(12438034276587152605)
XLA Ops:
  7.8 0.9 convert_reduce_fusion
  8.7 0.7 multiply_add_fusion
  9.4 2.3 %convolution_convert_fusion = bf16[256,1792]{1,0:T(8,128)(2,1)} fusion(bf16[128,1024]{1,0:T(8,128)(2,1)} %param.6, bf16[128,768]{1,0:T(8,128)(2,1)} %param.5, s32[128]{0:T(128)S(1)} %multiply_add_fusion, pred[128]{0:T(512)(128)(4,1)S(1)} %iota_compare_fusion.2), kind=kOutput, calls=%fused_computation | convolution fusion | flops 118882304 | bytes 1376896 | tf_op jit(solution)/shard_map/dot_general | solution.py:28
  11.7 7.3 %all-to-all-start = ((bf16[8,32,1792]{2,1,0:T(8,128)(2,1)}), bf16[8,32,1792]{2,1,0:T(8,128)(2,1)S(1)}, u32[]{:S(2)}, u32[]{:S(2)}) async-start(bf16[8,32,1792]{2,1,0:T(8,128)(2,1)} %bitcast.2), calls=%async_computation | async-start | bytes 1835008 | tf_op jit(solution)/shard_map/all_to_all | solution.py:33
  19.1 0.0 all-gather.2.cloned.1.call-start
  19.1 0.0 copy-done.2
  19.1 0.6 copy.18
  19.7 0.0 all-gather.2.cloned.1.call-update
  19.8 15.8 %all-to-all-done = bf16[8,32,1792]{2,1,0:T(8,128)(2,1)S(1)} async-done(((bf16[8,32,1792]{2,1,0:T(8,128)(2,1)}), bf16[8,32,1792]{2,1,0:T(8,128)(2,1)S(1)}, u32[]{:S(2)}, u32[]{:S(2)}) %all-to-all-start) | async-done | bytes 917536 | tf_op jit(solution)/shard_map/all_to_all | solution.py:33
  35.6 0.2 copy.16
  35.8 0.1 reshape.47
  36.0 0.1 reshape.48
  36.1 0.4 copy-done
  36.5 0.6 fusion.1
  37.1 17.2 %all_to_all.25 = f32[2,384,1024]{2,1,0:T(8,128)S(1)} all-to-all(f32[2,384,1024]{2,1,0:T(8,128)S(1)} %fusion.1), channel_id=1, replica_groups=mesh['expert'=8,'y'=8,'z'=8,'c'=2] {'c'}, dimensions={0} | all-to-all | bytes 6291456 | tf_op jit(solution)/shard_map/all_to_all | solution.py:43
  54.3 1.6 reduce_sum.37
  55.9 57.2 %all_to_all.26 = f32[8,48,1024]{2,1,0:T(8,128)S(1)} all-to-all(f32[8,48,1024]{2,1,0:T(8,128)} %bitcast.26), channel_id=1, replica_groups=mesh['expert'=8,'y'=8,'z'=8,'c'=2] {'z'}, dimensions={0} | all-to-all | bytes 3145728 | tf_op jit(solution)/shard_map/all_to_all | solution.py:43
  113.0 0.1 reduce_sum.38
  113.1 0.7 reshape.50
  113.9 7.5 %all-to-all-start.3 = ((f32[8,6,1024]{2,1,0:T(8,128)}), f32[8,6,1024]{2,1,0:T(8,128)S(1)}, u32[]{:S(2)}, u32[]{:S(2)}) async-start(f32[8,6,1024]{2,1,0:T(8,128)} %reshape.50), calls=%async_computation.3 | async-start | bytes 524288 | tf_op jit(solution)/shard_map/all_to_all | solution.py:43
  121.4 12.2 %all-gather.2.cloned.1.call-done = bf16[1,768,1024]{2,0,1:T(2,128)(2,1)} async-done(((bf16[1,6,1024]{2,0,1:T(2,128)(2,1)}), bf16[1,768,1024]{2,0,1:T(2,128)(2,1)}) %all-gather.2.cloned.1.call-update) | async-done | bytes 1572880 | tf_op jit(solution)/shard_map/all_gather | solution.py:32
  133.6 2.5 %copy.21 = bf16[1,768,1024]{2,1,0:T(8,128)(2,1)S(1)} copy(bf16[1,768,1024]{2,0,1:T(2,128)(2,1)} %all-gather.2.cloned.1.call-done) | data formatting | bytes 3145728
  136.1 0.0 all-to-all-done.3
  136.1 0.0 copy-done.1
  136.2 0.6 convolution_convert_fusion.1
  136.7 0.6 convolution_convert_fusion.2
  137.4 1.0 pad_maximum_fusion
  138.4 4.5 %all-to-all-start.4 = ((bf16[8,32,1792]{2,1,0:T(8,128)(2,1)}), bf16[8,32,1792]{2,1,0:T(8,128)(2,1)S(1)}, u32[]{:S(2)}, u32[]{:S(2)}) async-start(bf16[8,32,1792]{2,1,0:T(8,128)(2,1)} %bitcast.9), calls=%async_computation.4 | async-start | bytes 1835008 | tf_op jit(solution)/shard_map/all_to_all | solution.py:52
  142.9 0.6 broadcast_in_dim.2
  143.5 25.8 %all-to-all-done.4 = bf16[8,32,1792]{2,1,0:T(8,128)(2,1)S(1)} async-done(((bf16[8,32,1792]{2,1,0:T(8,128)(2,1)}), bf16[8,32,1792]{2,1,0:T(8,128)(2,1)S(1)}, u32[]{:S(2)}, u32[]{:S(2)}) %all-to-all-start.4) | async-done | bytes 917536 | tf_op jit(solution)/shard_map/all_to_all | solution.py:52
  169.3 1.0 convolution_convert_fusion.3
  170.2 0.9 convolution_convert_fusion.4
  (7 shorter events, 0.1 us)
Async XLA Ops:
  9.4 9.7 %copy-start.2 = (bf16[1,6,1024]{2,1,0:T(8,128)(2,1)S(1)}, bf16[1,6,1024]{2,1,0:T(8,128)(2,1)}, u32[]{:S(2)}) copy-start(bf16[1,6,1024]{2,1,0:T(8,128)(2,1)} %param.9) | copy-start | bytes 36868
  11.7 23.8 %all-to-all-start = ((bf16[8,32,1792]{2,1,0:T(8,128)(2,1)}), bf16[8,32,1792]{2,1,0:T(8,128)(2,1)S(1)}, u32[]{:S(2)}, u32[]{:S(2)}) async-start(bf16[8,32,1792]{2,1,0:T(8,128)(2,1)} %bitcast.2), calls=%async_computation | async-start | bytes 1835008 | tf_op jit(solution)/shard_map/all_to_all | solution.py:33
  19.1 114.6 %all-gather.2.cloned.1.call-start = ((), (), s32[]{:S(2)}) async-start(), calls=%async_computation.5 | async-start | bytes 3170304 | tf_op jit(solution)/shard_map/all_gather | solution.py:32
  35.6 1.0 copy-start
  113.9 22.2 %all-to-all-start.3 = ((f32[8,6,1024]{2,1,0:T(8,128)}), f32[8,6,1024]{2,1,0:T(8,128)S(1)}, u32[]{:S(2)}, u32[]{:S(2)}) async-start(f32[8,6,1024]{2,1,0:T(8,128)} %reshape.50), calls=%async_computation.3 | async-start | bytes 524288 | tf_op jit(solution)/shard_map/all_to_all | solution.py:43
  121.4 14.8 %copy-start.1 = (bf16[8,32,1792]{2,1,0:T(8,128)(2,1)S(1)}, bf16[8,32,1792]{2,1,0:T(8,128)(2,1)}, u32[]{:S(2)}) copy-start(bf16[8,32,1792]{2,1,0:T(8,128)(2,1)} %copy-done) | copy-start | bytes 2752516
  138.4 30.9 %all-to-all-start.4 = ((bf16[8,32,1792]{2,1,0:T(8,128)(2,1)}), bf16[8,32,1792]{2,1,0:T(8,128)(2,1)S(1)}, u32[]{:S(2)}, u32[]{:S(2)}) async-start(bf16[8,32,1792]{2,1,0:T(8,128)(2,1)} %bitcast.9), calls=%async_computation.4 | async-start | bytes 1835008 | tf_op jit(solution)/shard_map/all_to_all | solution.py:52
Sparse Core Ops, SparseCore 0:
  24.7 108.8 all-gather.1

commit v9 on v8

--- a/solution.py
+++ b/solution.py
@@ -56,12 +56,11 @@
         concat_axis=0,
         tiled=True,
     ).reshape(width, d + ff)
-    output = lax.dot_general(
-        placing, back[:, :d], (((0,), (0,)), ((), ())), preferred_element_type=jnp.float32
+    placed_back = lax.dot_general(
+        placing, back, (((0,), (0,)), ((), ())), preferred_element_type=jnp.float32
     ).astype(jnp.bfloat16)
-    hidden_grad = lax.dot_general(
-        placing, back[:, d:], (((0,), (0,)), ((), ())), preferred_element_type=jnp.float32
-    ).astype(jnp.bfloat16)
+    output = placed_back[:, :d]
+    hidden_grad = placed_back[:, d:]
     return (output, hidden_grad, summed[None])
 
 

time: 179 us -> 178 us (level)
  no operation moved by 1% of the time
where the time goes in v9:
time: 178 us
  blocking collectives  74.4 us (42%)
  waiting for transfers between devices  53.8 us (30%)
  starting transfers between devices  19.4 us (11%)
  between operations  14.8 us (8%)
  local copies, waits for them, and re-layouts  6.82 us (4%)
  matrix products  4.44 us (2%)
  other arithmetic  4.24 us (2%)
    all_to_all x2, blocking collectives, on_device(): lax.all_to_all(summed.reshape(n, summed.shape[0] // n, d), axis, split_ax...  74.4 us
    all_to_all x1, waiting for transfers between devices, on_device(): lax.all_to_all(jnp.concatenate([y_rows, dh_rows], axis=1).reshape(groups,...  25.8 us
    all_to_all x1, waiting for transfers between devices, on_device(): lax.all_to_all(send, 'expert', split_axis=0, concat_axis=0, tiled=True)  15.8 us
    all_gather x1, waiting for transfers between devices, on_device(): weight = lax.all_gather(down_weight, DP, axis=1, tiled=True)[0]  12.2 us
    all_to_all x1, starting transfers between devices, on_device(): lax.all_to_all(summed.reshape(n, summed.shape[0] // n, d), axis, split_ax...  7.51 us
    all_to_all x1, starting transfers between devices, on_device(): lax.all_to_all(send, 'expert', split_axis=0, concat_axis=0, tiled=True)  7.31 us
    all_to_all x1, starting transfers between devices, on_device(): lax.all_to_all(jnp.concatenate([y_rows, dh_rows], axis=1).reshape(groups,...  4.53 us
  transfers between devices with their start and end apart: 4, of which 3 were waited for; matrix products, arithmetic and copies ran while one was open for 4% of the time, Pallas kernels for 0%

profile of v9, /device:TPU:1, one launch (start us, length us, event | category | flops | bytes accessed | tf_op | source)
XLA Modules:
  0.0 177.9 jit_solution(3054853741163228511)
XLA Ops:
  7.8 0.9 convert_reduce_fusion
  8.7 0.7 multiply_add_fusion
  9.4 2.3 %convolution_convert_fusion = bf16[256,1792]{1,0:T(8,128)(2,1)} fusion(bf16[128,1024]{1,0:T(8,128)(2,1)} %param.6, bf16[128,768]{1,0:T(8,128)(2,1)} %param.5, s32[128]{0:T(128)S(1)} %multiply_add_fusion, pred[128]{0:T(512)(128)(4,1)S(1)} %iota_compare_fusion.2), kind=kOutput, calls=%fused_computation | convolution fusion | flops 118882304 | bytes 1376896 | tf_op jit(solution)/shard_map/dot_general | solution.py:28
  11.7 7.3 %all-to-all-start = ((bf16[8,32,1792]{2,1,0:T(8,128)(2,1)}), bf16[8,32,1792]{2,1,0:T(8,128)(2,1)S(1)}, u32[]{:S(2)}, u32[]{:S(2)}) async-start(bf16[8,32,1792]{2,1,0:T(8,128)(2,1)} %bitcast.2), calls=%async_computation | async-start | bytes 1835008 | tf_op jit(solution)/shard_map/all_to_all | solution.py:33
  19.1 0.0 all-gather.2.cloned.1.call-start
  19.1 0.6 copy.18
  19.7 0.0 all-gather.2.cloned.1.call-update
  19.8 15.8 %all-to-all-done = bf16[8,32,1792]{2,1,0:T(8,128)(2,1)S(1)} async-done(((bf16[8,32,1792]{2,1,0:T(8,128)(2,1)}), bf16[8,32,1792]{2,1,0:T(8,128)(2,1)S(1)}, u32[]{:S(2)}, u32[]{:S(2)}) %all-to-all-start) | async-done | bytes 917536 | tf_op jit(solution)/shard_map/all_to_all | solution.py:33
  35.6 0.2 copy.16
  35.8 0.1 reshape.47
  36.0 0.1 reshape.48
  36.1 0.4 copy-done
  36.5 0.6 fusion
  37.1 17.2 %all_to_all.25 = f32[2,384,1024]{2,1,0:T(8,128)S(1)} all-to-all(f32[2,384,1024]{2,1,0:T(8,128)S(1)} %fusion), channel_id=1, replica_groups=mesh['expert'=8,'y'=8,'z'=8,'c'=2] {'c'}, dimensions={0} | all-to-all | bytes 6291456 | tf_op jit(solution)/shard_map/all_to_all | solution.py:43
  54.3 1.6 reduce_sum.37
  55.9 57.2 %all_to_all.26 = f32[8,48,1024]{2,1,0:T(8,128)S(1)} all-to-all(f32[8,48,1024]{2,1,0:T(8,128)} %bitcast.27), channel_id=1, replica_groups=mesh['expert'=8,'y'=8,'z'=8,'c'=2] {'z'}, dimensions={0} | all-to-all | bytes 3145728 | tf_op jit(solution)/shard_map/all_to_all | solution.py:43
  113.0 0.1 reduce_sum.38
  113.1 0.7 reshape.50
  113.9 7.5 %all-to-all-start.3 = ((f32[8,6,1024]{2,1,0:T(8,128)}), f32[8,6,1024]{2,1,0:T(8,128)S(1)}, u32[]{:S(2)}, u32[]{:S(2)}) async-start(f32[8,6,1024]{2,1,0:T(8,128)} %reshape.50), calls=%async_computation.3 | async-start | bytes 524288 | tf_op jit(solution)/shard_map/all_to_all | solution.py:43
  121.4 12.2 %all-gather.2.cloned.1.call-done = bf16[1,768,1024]{2,0,1:T(2,128)(2,1)} async-done(((bf16[1,6,1024]{2,0,1:T(2,128)(2,1)}), bf16[1,768,1024]{2,0,1:T(2,128)(2,1)}) %all-gather.2.cloned.1.call-update) | async-done | bytes 1572880 | tf_op jit(solution)/shard_map/all_gather | solution.py:32
  133.6 2.5 %copy.21 = bf16[1,768,1024]{2,1,0:T(8,128)(2,1)S(1)} copy(bf16[1,768,1024]{2,0,1:T(2,128)(2,1)} %all-gather.2.cloned.1.call-done) | data formatting | bytes 3145728
  136.1 0.0 all-to-all-done.3
  136.1 0.0 copy-done.1
  136.2 0.6 convolution_convert_fusion.2
  136.7 0.6 convolution_convert_fusion.3
  137.4 1.0 pad_maximum_fusion
  138.4 4.5 %all-to-all-start.4 = ((bf16[8,32,1792]{2,1,0:T(8,128)(2,1)}), bf16[8,32,1792]{2,1,0:T(8,128)(2,1)S(1)}, u32[]{:S(2)}, u32[]{:S(2)}) async-start(bf16[8,32,1792]{2,1,0:T(8,128)(2,1)} %bitcast.9), calls=%async_computation.4 | async-start | bytes 1835008 | tf_op jit(solution)/shard_map/all_to_all | solution.py:52
  142.9 0.6 broadcast_in_dim.2
  143.5 25.8 %all-to-all-done.4 = bf16[8,32,1792]{2,1,0:T(8,128)(2,1)S(1)} async-done(((bf16[8,32,1792]{2,1,0:T(8,128)(2,1)}), bf16[8,32,1792]{2,1,0:T(8,128)(2,1)S(1)}, u32[]{:S(2)}, u32[]{:S(2)}) %all-to-all-start.4) | async-done | bytes 917536 | tf_op jit(solution)/shard_map/all_to_all | solution.py:52
  169.3 0.3 convolution_convert_fusion.1
  169.6 0.7 slice.18
  170.3 0.7 slice.19
  (8 shorter events, 0.1 us)
Async XLA Ops:
  9.4 9.7 %copy-start.2 = (bf16[1,6,1024]{2,1,0:T(8,128)(2,1)S(1)}, bf16[1,6,1024]{2,1,0:T(8,128)(2,1)}, u32[]{:S(2)}) copy-start(bf16[1,6,1024]{2,1,0:T(8,128)(2,1)} %param.9) | copy-start | bytes 36868
  11.7 23.8 %all-to-all-start = ((bf16[8,32,1792]{2,1,0:T(8,128)(2,1)}), bf16[8,32,1792]{2,1,0:T(8,128)(2,1)S(1)}, u32[]{:S(2)}, u32[]{:S(2)}) async-start(bf16[8,32,1792]{2,1,0:T(8,128)(2,1)} %bitcast.2), calls=%async_computation | async-start | bytes 1835008 | tf_op jit(solution)/shard_map/all_to_all | solution.py:33
  19.1 114.6 %all-gather.2.cloned.1.call-start = ((), (), s32[]{:S(2)}) async-start(), calls=%async_computation.5 | async-start | bytes 3170304 | tf_op jit(solution)/shard_map/all_gather | solution.py:32
  35.6 1.0 copy-start
  113.9 22.2 %all-to-all-start.3 = ((f32[8,6,1024]{2,1,0:T(8,128)}), f32[8,6,1024]{2,1,0:T(8,128)S(1)}, u32[]{:S(2)}, u32[]{:S(2)}) async-start(f32[8,6,1024]{2,1,0:T(8,128)} %reshape.50), calls=%async_computation.3 | async-start | bytes 524288 | tf_op jit(solution)/shard_map/all_to_all | solution.py:43
  121.4 14.8 %copy-start.1 = (bf16[8,32,1792]{2,1,0:T(8,128)(2,1)S(1)}, bf16[8,32,1792]{2,1,0:T(8,128)(2,1)}, u32[]{:S(2)}) copy-start(bf16[8,32,1792]{2,1,0:T(8,128)(2,1)} %copy-done) | copy-start | bytes 2752516
  138.4 30.9 %all-to-all-start.4 = ((bf16[8,32,1792]{2,1,0:T(8,128)(2,1)}), bf16[8,32,1792]{2,1,0:T(8,128)(2,1)S(1)}, u32[]{:S(2)}, u32[]{:S(2)}) async-start(bf16[8,32,1792]{2,1,0:T(8,128)(2,1)} %bitcast.9), calls=%async_computation.4 | async-start | bytes 1835008 | tf_op jit(solution)/shard_map/all_to_all | solution.py:52
Sparse Core Ops, SparseCore 0:
  24.7 108.8 all-gather.1

commit v10 on v9

--- a/solution.py
+++ b/solution.py
@@ -29,7 +29,7 @@
         .astype(jnp.bfloat16)
         .reshape(groups, CAP, ff + d)
     )
-    weight = lax.all_gather(down_weight, DP, axis=1, tiled=True)[0]
+    weight_t = lax.all_gather(down_weight[0].T, DP, axis=1, tiled=True)
     recv = lax.all_to_all(send, "expert", split_axis=0, concat_axis=0, tiled=True).reshape(width, ff + d)
     h_rows = recv[:, :ff]
     g_rows = recv[:, ff:]
@@ -44,11 +44,11 @@
             summed.reshape(n, summed.shape[0] // n, d), axis, split_axis=0, concat_axis=0, tiled=True
         )
         summed = jnp.sum(parts, axis=0)
-    summed, weight = lax.optimization_barrier((summed, weight))
-    y_rows = jnp.dot(h_rows, weight, preferred_element_type=jnp.float32).astype(jnp.bfloat16)
-    dh_rows = lax.dot_general(
-        g_rows, weight, (((1,), (1,)), ((), ())), preferred_element_type=jnp.float32
+    summed, weight_t = lax.optimization_barrier((summed, weight_t))
+    y_rows = lax.dot_general(
+        h_rows, weight_t, (((1,), (1,)), ((), ())), preferred_element_type=jnp.float32
     ).astype(jnp.bfloat16)
+    dh_rows = jnp.dot(g_rows, weight_t, preferred_element_type=jnp.float32).astype(jnp.bfloat16)
     back = lax.all_to_all(
         jnp.concatenate([y_rows, dh_rows], axis=1).reshape(groups, CAP, d + ff),
         "expert",

time: 178 us -> 177 us (level)
    all_gather x1, waiting for transfers between devices: 12.2 us -> 10.4 us  [on_device(): weight_t = lax.all_gather(down_weight[0].T, DP, axis=1, tiled=True)]
where the time goes in v10:
time: 177 us; the launch traced here: 176 us
  blocking collectives  73.5 us (42%)
  waiting for transfers between devices  52.6 us (30%)
  starting transfers between devices  20.4 us (12%)
  between operations  14.8 us (8%)
  local copies, waits for them, and re-layouts  6.27 us (4%)
  matrix products  4.42 us (2%)
  other arithmetic  4.23 us (2%)
    all_to_all x2, blocking collectives, on_device(): lax.all_to_all(summed.reshape(n, summed.shape[0] // n, d), axis, split_ax...  73.5 us
    all_to_all x1, waiting for transfers between devices, on_device(): lax.all_to_all(jnp.concatenate([y_rows, dh_rows], axis=1).reshape(groups,...  25.8 us
    all_to_all x1, waiting for transfers between devices, on_device(): lax.all_to_all(send, 'expert', split_axis=0, concat_axis=0, tiled=True)  15.8 us
    all_gather x1, waiting for transfers between devices, on_device(): weight_t = lax.all_gather(down_weight[0].T, DP, axis=1, tiled=True)  10.4 us
    all_to_all x1, starting transfers between devices, on_device(): lax.all_to_all(summed.reshape(n, summed.shape[0] // n, d), axis, split_ax...  7.46 us
    all_to_all x1, starting transfers between devices, on_device(): lax.all_to_all(send, 'expert', split_axis=0, concat_axis=0, tiled=True)  7.31 us
    all_to_all x1, starting transfers between devices, on_device(): lax.all_to_all(jnp.concatenate([y_rows, dh_rows], axis=1).reshape(groups,...  5.57 us
  transfers between devices with their start and end apart: 4, of which 3 were waited for; matrix products, arithmetic and copies ran while one was open for 4% of the time, Pallas kernels for 0%

profile of v10, /device:TPU:1, one launch (start us, length us, event | category | flops | bytes accessed | tf_op | source)
XLA Modules:
  0.0 176.2 jit_solution(3041090619213534369)
XLA Ops:
  7.8 0.9 convert_reduce_fusion
  8.7 0.7 multiply_add_fusion
  9.4 2.3 %convolution_convert_fusion = bf16[256,1792]{1,0:T(8,128)(2,1)} fusion(bf16[128,1024]{1,0:T(8,128)(2,1)} %param.6, bf16[128,768]{1,0:T(8,128)(2,1)} %param.5, s32[128]{0:T(128)S(1)} %multiply_add_fusion, pred[128]{0:T(512)(128)(4,1)S(1)} %iota_compare_fusion.2), kind=kOutput, calls=%fused_computation | convolution fusion | flops 118882304 | bytes 1376896 | tf_op jit(solution)/shard_map/dot_general | solution.py:28
  11.7 7.3 %all-to-all-start = ((bf16[8,32,1792]{2,1,0:T(8,128)(2,1)}), bf16[8,32,1792]{2,1,0:T(8,128)(2,1)S(1)}, u32[]{:S(2)}, u32[]{:S(2)}) async-start(bf16[8,32,1792]{2,1,0:T(8,128)(2,1)} %bitcast.2), calls=%async_computation | async-start | bytes 1835008 | tf_op jit(solution)/shard_map/all_to_all | solution.py:33
  19.0 0.0 all-gather.3.cloned.1.call-start
  19.1 0.7 all-gather.3.cloned.1.call-update
  19.8 15.8 %all-to-all-done = bf16[8,32,1792]{2,1,0:T(8,128)(2,1)S(1)} async-done(((bf16[8,32,1792]{2,1,0:T(8,128)(2,1)}), bf16[8,32,1792]{2,1,0:T(8,128)(2,1)S(1)}, u32[]{:S(2)}, u32[]{:S(2)}) %all-to-all-start) | async-done | bytes 917536 | tf_op jit(solution)/shard_map/all_to_all | solution.py:33
  35.5 0.0 copy-start
  35.6 0.2 copy.12
  35.7 0.1 reshape.47
  35.9 0.1 reshape.48
  36.1 0.4 copy-done
  36.5 0.6 fusion
  37.0 17.2 %all_to_all.25 = f32[2,384,1024]{2,1,0:T(8,128)S(1)} all-to-all(f32[2,384,1024]{2,1,0:T(8,128)S(1)} %fusion), channel_id=1, replica_groups=mesh['expert'=8,'y'=8,'z'=8,'c'=2] {'c'}, dimensions={0} | all-to-all | bytes 6291456 | tf_op jit(solution)/shard_map/all_to_all | solution.py:43
  54.2 1.5 reduce_sum.37
  55.8 56.3 %all_to_all.26 = f32[8,48,1024]{2,1,0:T(8,128)S(1)} all-to-all(f32[8,48,1024]{2,1,0:T(8,128)} %bitcast.25), channel_id=1, replica_groups=mesh['expert'=8,'y'=8,'z'=8,'c'=2] {'z'}, dimensions={0} | all-to-all | bytes 3145728 | tf_op jit(solution)/shard_map/all_to_all | solution.py:43
  112.0 0.1 reduce_sum.38
  112.1 0.7 reshape.50
  112.9 7.5 %all-to-all-start.3 = ((f32[8,6,1024]{2,1,0:T(8,128)}), f32[8,6,1024]{2,1,0:T(8,128)S(1)}, u32[]{:S(2)}, u32[]{:S(2)}) async-start(f32[8,6,1024]{2,1,0:T(8,128)} %reshape.50), calls=%async_computation.3 | async-start | bytes 524288 | tf_op jit(solution)/shard_map/all_to_all | solution.py:43
  120.3 10.4 %all-gather.3.cloned.1.call-done = bf16[128,6,1024]{2,1,0:T(8,128)(2,1)} async-done(((bf16[1,6,1024]{2,1,0:T(8,128)(2,1)}), bf16[128,6,1024]{2,1,0:T(8,128)(2,1)}) %all-gather.3.cloned.1.call-update) | async-done | bytes 1572880 | tf_op jit(solution)/shard_map/all_gather | solution.py:32
  130.8 2.6 %reshape.54 = bf16[768,1024]{1,0:T(8,128)(2,1)S(1)} reshape(bf16[128,6,1024]{2,1,0:T(8,128)(2,1)} %all-gather.3.cloned.1.call-done) | data formatting | bytes 3145728
  133.4 0.0 all-to-all-done.3
  133.4 0.0 copy-done.1
  133.4 0.6 convolution_convert_fusion.2
  134.0 0.6 convolution_convert_fusion.3
  134.6 1.0 pad_maximum_fusion
  135.6 5.6 %all-to-all-start.4 = ((bf16[8,32,1792]{2,1,0:T(8,128)(2,1)}), bf16[8,32,1792]{2,1,0:T(8,128)(2,1)S(1)}, u32[]{:S(2)}, u32[]{:S(2)}) async-start(bf16[8,32,1792]{2,1,0:T(8,128)(2,1)} %bitcast.10), calls=%async_computation.4 | async-start | bytes 1835008 | tf_op jit(solution)/shard_map/all_to_all | solution.py:52
  141.2 0.6 broadcast_in_dim.2
  141.8 25.8 %all-to-all-done.4 = bf16[8,32,1792]{2,1,0:T(8,128)(2,1)S(1)} async-done(((bf16[8,32,1792]{2,1,0:T(8,128)(2,1)}), bf16[8,32,1792]{2,1,0:T(8,128)(2,1)S(1)}, u32[]{:S(2)}, u32[]{:S(2)}) %all-to-all-start.4) | async-done | bytes 917536 | tf_op jit(solution)/shard_map/all_to_all | solution.py:52
  167.6 0.3 convolution_convert_fusion.1
  167.9 0.7 slice.18
  168.6 0.7 slice.19
  (5 shorter events, 0.1 us)
Async XLA Ops:
  11.7 23.8 %all-to-all-start = ((bf16[8,32,1792]{2,1,0:T(8,128)(2,1)}), bf16[8,32,1792]{2,1,0:T(8,128)(2,1)S(1)}, u32[]{:S(2)}, u32[]{:S(2)}) async-start(bf16[8,32,1792]{2,1,0:T(8,128)(2,1)} %bitcast.2), calls=%async_computation | async-start | bytes 1835008 | tf_op jit(solution)/shard_map/all_to_all | solution.py:33
  19.0 111.7 %all-gather.3.cloned.1.call-start = ((), (), s32[]{:S(2)}) async-start(), calls=%async_computation.5 | async-start | bytes 2113536 | tf_op jit(solution)/shard_map/all_gather | solution.py:32
  35.5 0.9 copy-start
  112.9 20.5 %all-to-all-start.3 = ((f32[8,6,1024]{2,1,0:T(8,128)}), f32[8,6,1024]{2,1,0:T(8,128)S(1)}, u32[]{:S(2)}, u32[]{:S(2)}) async-start(f32[8,6,1024]{2,1,0:T(8,128)} %reshape.50), calls=%async_computation.3 | async-start | bytes 524288 | tf_op jit(solution)/shard_map/all_to_all | solution.py:43
  120.3 13.1 %copy-start.1 = (bf16[8,32,1792]{2,1,0:T(8,128)(2,1)S(1)}, bf16[8,32,1792]{2,1,0:T(8,128)(2,1)}, u32[]{:S(2)}) copy-start(bf16[8,32,1792]{2,1,0:T(8,128)(2,1)} %copy-done) | copy-start | bytes 2752516
  135.6 32.0 %all-to-all-start.4 = ((bf16[8,32,1792]{2,1,0:T(8,128)(2,1)}), bf16[8,32,1792]{2,1,0:T(8,128)(2,1)S(1)}, u32[]{:S(2)}, u32[]{:S(2)}) async-start(bf16[8,32,1792]{2,1,0:T(8,128)(2,1)} %bitcast.10), calls=%async_computation.4 | async-start | bytes 1835008 | tf_op jit(solution)/shard_map/all_to_all | solution.py:52
Sparse Core Ops, SparseCore 0:
  24.2 106.5 all-gather.2
